TPU v7x, 256 devices: a whole 4x4x8 slice. The times are simulated.
256 devices in a mesh: wide: 32 (over x, y, z_lo), narrow: 8 (over z_hi, core).
Axes of the slice: x: 4, y: 4, z: 8 (z_hi: 4, z_lo: 2; z = z_hi * 2 + z_lo), core: 2. Of those that a mesh axis runs over, the one named last changes fastest.
Arguments:
- r_matrix: bfloat16 [10240, 102400], P('narrow', 'wide'), may hold values from -0.01953125 to 0.01953125
- cmm_panel: bfloat16 [102400, 1280], P('wide', 'narrow'), may hold values from -18 to 18
- ctm_panel: bfloat16 [10240, 1280], P('narrow', 'wide'), may hold values from -18 to 18
- cee_in: float32 [10240, 10240], P('wide', 'narrow'), may hold values from -2 to 2
Outputs:
- cee_out: float32 [10240, 10240], P('wide', 'narrow')
All inputs are finite; a program needn't handle non-finite values.
Results may differ from a plain program's by a relative error of at most 0.0022.
Values may be sent and summed in bfloat16 or wider, within the bound.
No kernel may reach another device: no remote copies, remote signals or barrier semaphores. Data moves between devices by JAX's collectives and lax.ppermute only.
A program may use at most 128 MiB of HBM per device.

v0:
```python
import jax
import jax.numpy as jnp
from jax import lax
from jax.sharding import PartitionSpec as P


def spread(value, axis, root):
    mine = lax.axis_index(axis) == root
    return lax.psum(jnp.where(mine, value, jnp.zeros_like(value)), axis)


def per_device(r_matrix, cmm_panel, ctm_panel, cee_in):
    slope_rows = r_matrix.shape[0]
    tile_rows = cee_in.shape[0]
    panel_width = ctm_panel.shape[1]
    r_panel = r_matrix[:, :panel_width]
    z_part = jnp.dot(
        r_matrix,
        lax.all_gather(cmm_panel, "narrow", axis=1, tiled=True),
        preferred_element_type=jnp.float32,
    )
    z_mine = lax.psum_scatter(z_part, "wide", scatter_dimension=1, tiled=True)
    a_mine = (z_mine - ctm_panel.astype(jnp.float32)).astype(jnp.bfloat16)
    a_whole, r_whole, c_whole = (
        lax.all_gather(a_mine, "wide", axis=1, tiled=True),
        lax.all_gather(r_panel, "wide", axis=1, tiled=True),
        lax.all_gather(ctm_panel, "wide", axis=1, tiled=True),
    )
    wide_index = lax.axis_index("wide")
    narrow_index = lax.axis_index("narrow")
    owner = wide_index * tile_rows // slope_rows
    offset = jnp.clip(wide_index * tile_rows - narrow_index * slope_rows, 0, slope_rows - tile_rows)
    a_rows = lax.dynamic_slice_in_dim(a_whole, offset, tile_rows, 0)
    r_rows = lax.dynamic_slice_in_dim(r_whole, offset, tile_rows, 0)
    left_rows = jnp.concatenate([a_rows, r_rows], axis=1)
    left_rows = spread(left_rows, "narrow", owner)
    right_cols = jnp.concatenate([r_whole, -c_whole], axis=1)
    update = lax.dot_general(
        left_rows, right_cols, (((1,), (1,)), ((), ())), preferred_element_type=jnp.float32
    )
    return cee_in + update


def solution(mesh):
    placed = (P("narrow", "wide"), P("wide", "narrow"), P("narrow", "wide"), P("wide", "narrow"))
    return jax.shard_map(
        per_device, mesh=mesh, in_specs=placed, out_specs=P("wide", "narrow"), check_vma=False
    )
```

profile of v0, /device:TPU:42, one launch (start us, length us, event | category | flops | bytes accessed | tf_op | source)
XLA Modules:
  0.0 890.3 jit_solution(11240906440603850587)
XLA Ops:
  6.5 0.0 all-gather.5.cloned.1.call-start
  6.5 0.7 all-gather.5.cloned.1.call-update
  7.3 0.0 reduce-scatter.2.cloned.1.call-start
  7.3 89.8 %all-gather.5.cloned.1.call-done = bf16[3200,1280]{0,1:T(8,128)(2,1)} async-done(((bf16[3200,160]{0,1:T(8,128)(2,1)}), bf16[3200,1280]{0,1:T(8,128)(2,1)}) %all-gather.5.cloned.1.call-update) | async-done | bytes 8192016 | tf_op jit(solution)/shard_map/all_gather | solution.py:19
  97.1 17.7 %fusion.8 = f32[1280,1280]{0,1:T(8,128)} fusion(bf16[1280,3200]{1,0:T(8,128)(2,1)} %param.4, bf16[3200,1280]{0,1:T(8,128)(2,1)} %all-gather.5.cloned.1.call-done), kind=kOutput, calls=%fused_computation.10 | convolution fusion | flops 10485760000 | bytes 22937600 | tf_op jit(solution)/shard_map/dot_general | solution.py:17
  114.8 0.0 slice-start
  114.8 0.0 copy-start
  114.8 0.0 reduce-scatter.2.cloned.1.call-update
  114.9 0.0 all-gather.9.cloned.1.call-start
  114.9 0.9 slice-done
  115.8 0.8 copy.6
  116.6 0.0 all-gather.9.cloned.1.call-update
  116.6 0.0 all-gather.7.cloned.1.call-start
  116.7 159.5 %reduce-scatter.2.cloned.1.call-done = f32[1280,40]{0,1:T(8,128)} async-done(((f32[1280,1280]{0,1:T(8,128)}), f32[1280,40]{0,1:T(8,128)}) %reduce-scatter.2.cloned.1.call-update) | async-done | bytes 204816 | tf_op jit(solution)/shard_map/reduce_scatter | solution.py:22
  276.2 0.0 copy-done
  276.2 1.6 subtract_convert_fusion
  277.7 0.0 all-gather.7.cloned.1.call-update
  277.8 0.0 all-gather.11.cloned.1.call-start
  277.8 0.5 all-gather.11.cloned.1.call-update
  278.4 0.0 all-reduce.2.cloned.1.call-start
  278.4 165.1 %all-gather.9.cloned.1.call-done = bf16[1280,1280]{0,1:T(8,128)(2,1)} async-done(((bf16[1280,40]{0,1:T(8,128)(2,1)}), bf16[1280,1280]{0,1:T(8,128)(2,1)}) %all-gather.9.cloned.1.call-update) | async-done | bytes 3276816 | tf_op jit(solution)/shard_map/all_gather | solution.py:26
  443.5 1.6 constant_dynamic-slice_fusion
  445.1 163.1 %all-gather.7.cloned.1.call-done = bf16[1280,1280]{0,1:T(8,128)(2,1)} async-done(((bf16[1280,40]{0,1:T(8,128)(2,1)}), bf16[1280,1280]{0,1:T(8,128)(2,1)}) %all-gather.7.cloned.1.call-update) | async-done | bytes 3276816 | tf_op jit(solution)/shard_map/all_gather | solution.py:25
  608.2 1.6 constant_dynamic-slice_fusion.1
  609.8 1.8 maximum_select_fusion
  611.6 0.0 all-reduce.2.cloned.1.call-update
  611.6 161.3 %all-gather.11.cloned.1.call-done = bf16[1280,1280]{0,1:T(8,128)(2,1)} async-done(((bf16[1280,40]{0,1:T(8,128)(2,1)}), bf16[1280,1280]{0,1:T(8,128)(2,1)}) %all-gather.11.cloned.1.call-update) | async-done | bytes 3276816 | tf_op jit(solution)/shard_map/all_gather | solution.py:27
  772.9 2.5 neg.3
  775.4 101.6 %all-reduce.2.cloned.1.call-done = bf16[320,2560]{0,1:T(8,128)(2,1)} async-done(((bf16[320,2560]{0,1:T(8,128)(2,1)}), bf16[320,2560]{0,1:T(8,128)(2,1)}) %all-reduce.2.cloned.1.call-update) | async-done | bytes 1638416 | tf_op jit(solution)/shard_map/psum | solution.py:9
  877.0 6.5 fusion.4
Async XLA Ops:
  6.5 90.5 %all-gather.5.cloned.1.call-start = ((), (), s32[]{:S(2)}) async-start(), calls=%async_computation.1 | async-start | bytes 9216000 | tf_op jit(solution)/shard_map/all_gather | solution.py:19
  7.3 268.9 %reduce-scatter.2.cloned.1.call-start = ((), (), s32[]{:S(2)}) async-start(), calls=%async_computation.2 | async-start | bytes 6758400 | tf_op jit(solution)/shard_map/reduce_scatter | solution.py:22
  114.8 1.0 slice-start
  114.8 161.3 %copy-start = (bf16[1280,40]{0,1:T(8,128)(2,1)S(1)}, bf16[1280,40]{0,1:T(8,128)(2,1)}, u32[]{:S(2)}) copy-start(bf16[1280,40]{0,1:T(8,128)(2,1)} %param.6) | copy-start | bytes 307204
  114.9 328.7 %all-gather.9.cloned.1.call-start = ((), (), s32[]{:S(2)}) async-start(), calls=%async_computation.4 | async-start | bytes 3379200 | tf_op jit(solution)/shard_map/all_gather | solution.py:26
  116.6 491.6 %all-gather.7.cloned.1.call-start = ((), (), s32[]{:S(2)}) async-start(), calls=%async_computation.3 | async-start | bytes 3379200 | tf_op jit(solution)/shard_map/all_gather | solution.py:25
  277.8 495.1 %all-gather.11.cloned.1.call-start = ((), (), s32[]{:S(2)}) async-start(), calls=%async_computation.6 | async-start | bytes 3379200 | tf_op jit(solution)/shard_map/all_gather | solution.py:27
  278.4 598.6 %all-reduce.2.cloned.1.call-start = ((), (), s32[]{:S(2)}) async-start(), calls=%async_computation.5 | async-start | bytes 3932160 | tf_op jit(solution)/shard_map/psum | solution.py:9
Sparse Core Ops, SparseCore 0:
  9.2 87.8 all-gather.4
  115.0 161.1 reduce-scatter.1
  278.0 165.5 all-gather.8
  445.2 163.0 all-gather.6
  609.9 163.0 all-gather.10
  775.5 101.4 all-reduce.1
where the time goes:
time: 892 us; the launch traced here: 890 us
  waiting for transfers between devices  842 us (94%)
  matrix products  24.2 us (3%)
  between operations  13.5 us (2%)
    all_gather x1, waiting for transfers between devices, per_device(): lax.all_gather(r_panel, 'wide', axis=1, tiled=True)  165 us
    all_gather x1, waiting for transfers between devices, per_device(): lax.all_gather(a_mine, 'wide', axis=1, tiled=True)  163 us
    all_gather x1, waiting for transfers between devices, per_device(): lax.all_gather(ctm_panel, 'wide', axis=1, tiled=True)  161 us
    reduce_scatter x1, waiting for transfers between devices, per_device(): z_mine = lax.psum_scatter(z_part, 'wide', scatter_dimension=1, tiled=True)  159 us
    psum x1, waiting for transfers between devices, spread(): return lax.psum(jnp.where(mine, value, jnp.zeros_like(value)), axis)  102 us
    all_gather x1, waiting for transfers between devices, per_device(): lax.all_gather(cmm_panel, 'narrow', axis=1, tiled=True)  89.8 us
  transfers between devices with their start and end apart: 6, of which 6 were waited for; matrix products, arithmetic and copies ran while one was open for 1% of the time, Pallas kernels for 0%

commit v1 on v0

v1 whole, which is shorter than its diff:
```python
import jax
import jax.numpy as jnp
from jax import lax
from jax.sharding import PartitionSpec as P


def per_device(r_matrix, cmm_panel, ctm_panel, cee_in, n_wide, n_narrow):
    slope_rows = r_matrix.shape[0]
    tile_rows = cee_in.shape[0]
    panel_width = ctm_panel.shape[1]
    piece = slope_rows // n_wide
    wide_index = lax.axis_index("wide")
    narrow_index = lax.axis_index("narrow")

    rc = jnp.concatenate([r_matrix[:, :panel_width], ctm_panel], axis=1)
    rc_all = lax.all_to_all(
        jnp.broadcast_to(rc[None], (n_wide,) + rc.shape), "wide", 0, 0, tiled=True
    )

    cmm_full = lax.all_gather(cmm_panel, "narrow", axis=1, tiled=True)
    z_part = jnp.dot(r_matrix, cmm_full, preferred_element_type=jnp.float32)

    z_recv = lax.all_to_all(
        z_part.reshape(n_wide, piece, z_part.shape[1]), "wide", 0, 0, tiled=True
    )
    z_mine = jnp.sum(z_recv, axis=0).reshape(piece, n_wide, panel_width)
    rc_rows = lax.dynamic_slice_in_dim(rc_all, wide_index * piece, piece, 1)
    rc_rows = jnp.transpose(rc_rows, (1, 0, 2))
    a_piece = (z_mine - rc_rows[:, :, panel_width:].astype(jnp.float32)).astype(jnp.bfloat16)
    left_piece = jnp.concatenate([a_piece, -rc_rows[:, :, :panel_width]], axis=2)

    blocks = n_wide // n_narrow
    perm = []
    for w in range(n_wide):
        for n in range(n_narrow):
            perm.append((w * n_narrow + n, (n * blocks + w // n_narrow) * n_narrow + w % n_narrow))
    left_piece = lax.ppermute(left_piece, ("wide", "narrow"), perm)
    left_rows = lax.all_gather(left_piece, "narrow", axis=0, tiled=True)

    update = lax.dot_general(
        left_rows, rc_all, (((1, 2), (0, 2)), ((), ())), preferred_element_type=jnp.float32
    )
    return cee_in + update


def solution(mesh):
    n_wide, n_narrow = mesh.shape["wide"], mesh.shape["narrow"]
    placed = (P("narrow", "wide"), P("wide", "narrow"), P("narrow", "wide"), P("wide", "narrow"))

    def body(r_matrix, cmm_panel, ctm_panel, cee_in):
        return per_device(r_matrix, cmm_panel, ctm_panel, cee_in, n_wide, n_narrow)

    return jax.shard_map(
        body, mesh=mesh, in_specs=placed, out_specs=P("wide", "narrow"), check_vma=False
    )
```

time: 892 us -> 364 us (0.41)
  waiting for transfers between devices: 842 us -> 290 us
  starting transfers between devices: 0.2 us -> 20 us
    all_gather x4 -> x2, waiting for transfers between devices: 579 us -> 149 us  [the longest x1 109 us: per_device(): cmm_full = lax.all_gather(cmm_panel, 'narrow', axis=1, tiled=True)]
    reduce_scatter x1 -> x0, waiting for transfers between devices: 159 us -> none  [per_device(): z_mine = lax.psum_scatter(z_part, 'wide', scatter_dimension=1, tiled=True)]
    all_to_all x0 -> x2, waiting for transfers between devices: none -> 103 us  [the longest x1 89.1 us: per_device(): lax.all_to_all(z_part.reshape(n_wide, piece, z_part.shape[1]), 'wide', 0,...]
    psum x1 -> x0, waiting for transfers between devices: 102 us -> none  [spread(): return lax.psum(jnp.where(mine, value, jnp.zeros_like(value)), axis)]
    ppermute x0 -> x1, waiting for transfers between devices: none -> 36.7 us  [per_device(): left_piece = lax.ppermute(left_piece, ('wide', 'narrow'), perm)]
    all_to_all x0 -> x2, starting transfers between devices: none -> 18 us  [the longest x1 9.54 us: per_device(): lax.all_to_all(z_part.reshape(n_wide, piece, z_part.shape[1]), 'wide', 0,...]
  transfers between devices with their start and end apart: 6 -> 5, of which waited for: 6 -> 5; matrix products, arithmetic and copies ran while one was open for 1% -> 7% of each run, Pallas kernels for 0% -> 0%
where the time goes in v1:
time: 364 us; the launch traced here: 361 us
  waiting for transfers between devices  290 us (80%)
  matrix products  26.2 us (7%)
  starting transfers between devices  20 us (5%)
  between operations  13.5 us (4%)
  local copies, waits for them, and re-layouts  7.4 us (2%)
  other arithmetic  4.34 us (1%)
    all_gather x1, waiting for transfers between devices, per_device(): cmm_full = lax.all_gather(cmm_panel, 'narrow', axis=1, tiled=True)  109 us
    all_to_all x1, waiting for transfers between devices, per_device(): lax.all_to_all(z_part.reshape(n_wide, piece, z_part.shape[1]), 'wide', 0,...  89.1 us
    all_gather x1, waiting for transfers between devices, per_device(): left_rows = lax.all_gather(left_piece, 'narrow', axis=0, tiled=True)  40 us
    ppermute x1, waiting for transfers between devices, per_device(): left_piece = lax.ppermute(left_piece, ('wide', 'narrow'), perm)  36.7 us
    dot_general x1, matrix products, per_device(): z_part = jnp.dot(r_matrix, cmm_full, preferred_element_type=jnp.float32)  17.7 us
    all_to_all x1, waiting for transfers between devices, per_device(): lax.all_to_all(jnp.broadcast_to(rc[None], (n_wide,) + rc.shape), 'wide',...  14.3 us
    all_to_all x1, starting transfers between devices, per_device(): lax.all_to_all(z_part.reshape(n_wide, piece, z_part.shape[1]), 'wide', 0,...  9.54 us
    all_to_all x1, starting transfers between devices, per_device(): lax.all_to_all(jnp.broadcast_to(rc[None], (n_wide,) + rc.shape), 'wide',...  8.46 us
  transfers between devices with their start and end apart: 5, of which 5 were waited for; matrix products, arithmetic and copies ran while one was open for 7% of the time, Pallas kernels for 0%

profile of v1, /device:TPU:42, one launch (start us, length us, event | category | flops | bytes accessed | tf_op | source)
XLA Modules:
  0.0 360.9 jit_solution(10119718328729937901)
XLA Ops:
  6.5 0.0 all-gather.3.cloned.1.call-start
  6.5 0.7 all-gather.3.cloned.1.call-update
  7.3 1.0 slice.9
  8.3 0.2 copy.11
  8.4 0.9 pad_maximum_fusion.1
  9.3 3.1 broadcast_in_dim.2
  12.4 8.5 %all-to-all-start.1 = ((bf16[32,1280,80]{1,2,0:T(8,128)(2,1)}), bf16[32,1280,80]{1,2,0:T(8,128)(2,1)}, u32[]{:S(2)}, u32[]{:S(2)}) async-start(bf16[32,1280,80]{1,2,0:T(8,128)(2,1)} %broadcast_in_dim.2), calls=%async_computation.1 | async-start | bytes 13107200 | tf_op jit(solution)/shard_map/all_to_all | solution.py:16
  20.9 108.7 %all-gather.3.cloned.1.call-done = bf16[3200,1280]{0,1:T(8,128)(2,1)} async-done(((bf16[3200,160]{0,1:T(8,128)(2,1)}), bf16[3200,1280]{0,1:T(8,128)(2,1)}) %all-gather.3.cloned.1.call-update) | async-done | bytes 8192016 | tf_op jit(solution)/shard_map/all_gather | solution.py:20
  129.5 17.7 %fusion.2 = f32[1280,1280]{1,0:T(8,128)} fusion(bf16[1280,3200]{1,0:T(8,128)(2,1)} %param.4, bf16[3200,1280]{0,1:T(8,128)(2,1)} %all-gather.3.cloned.1.call-done), kind=kOutput, calls=%fused_computation.8 | convolution fusion | flops 10485760000 | bytes 22937600 | tf_op jit(solution)/shard_map/dot_general | solution.py:21
  147.3 14.3 %all-to-all-done.1 = bf16[32,1280,80]{1,2,0:T(8,128)(2,1)} async-done(((bf16[32,1280,80]{1,2,0:T(8,128)(2,1)}), bf16[32,1280,80]{1,2,0:T(8,128)(2,1)}, u32[]{:S(2)}, u32[]{:S(2)}) %all-to-all-start.1) | async-done | bytes 6553632 | tf_op jit(solution)/shard_map/all_to_all | solution.py:16
  161.6 9.5 %all-to-all-start = ((f32[32,40,1280]{2,1,0:T(8,128)}), f32[32,40,1280]{2,1,0:T(8,128)}, u32[]{:S(2)}, u32[]{:S(2)}) async-start(f32[32,40,1280]{2,1,0:T(8,128)} %bitcast.11), calls=%async_computation | async-start | bytes 13107200 | tf_op jit(solution)/shard_map/all_to_all | solution.py:23
  171.2 0.0 all-gather.5.cloned.1.call-start
  171.2 0.0 copy-start.1
  171.2 1.7 dynamic-slice_bitcast_fusion
  173.0 89.1 %all-to-all-done = f32[32,40,1280]{2,1,0:T(8,128)} async-done(((f32[32,40,1280]{2,1,0:T(8,128)}), f32[32,40,1280]{2,1,0:T(8,128)}, u32[]{:S(2)}, u32[]{:S(2)}) %all-to-all-start) | async-done | bytes 6553632 | tf_op jit(solution)/shard_map/all_to_all | solution.py:23
  262.1 3.2 reduce_sum.9
  265.3 0.2 copy.7
  265.5 0.1 subtract_convert_fusion
  265.6 0.1 pad_maximum_fusion
  265.7 0.5 copy.9
  266.3 1.9 collective-permute-start
  268.2 36.7 %collective-permute-done = bf16[40,32,80]{2,1,0:T(8,128)(2,1)S(1)} collective-permute-done((bf16[40,32,80]{2,1,0:T(8,128)(2,1)S(1)}, bf16[40,32,80]{2,1,0:T(8,128)(2,1)S(1)}, u32[]{:S(2)}, u32[]{:S(2)}) %collective-permute-start) | collective-permute-done | bytes 204832 | tf_op jit(solution)/shard_map/ppermute | solution.py:37
  304.9 0.0 copy-start
  304.9 0.7 copy-done
  305.6 0.0 all-gather.5.cloned.1.call-update
  305.7 40.0 %all-gather.5.cloned.1.call-done = bf16[320,32,80]{2,1,0:T(8,128)(2,1)} async-done(((bf16[40,32,80]{2,1,0:T(8,128)(2,1)}), bf16[320,32,80]{2,1,0:T(8,128)(2,1)}) %all-gather.5.cloned.1.call-update) | async-done | bytes 1638416 | tf_op jit(solution)/shard_map/all_gather | solution.py:38
  345.7 0.0 copy-done.1
  345.7 8.4 %fusion = f32[320,1280]{1,0:T(8,128)} fusion(f32[320,1280]{1,0:T(8,128)S(1)} %copy-done.1, bf16[32,1280,80]{1,2,0:T(8,128)(2,1)} %all-to-all-done.1, bf16[320,32,80]{2,1,0:T(8,128)(2,1)} %all-gather.5.cloned.1.call-done), kind=kOutput, calls=%fused_computation.1 | convolution fusion | flops 2097561600 | bytes 11468800 | tf_op jit(solution)/shard_map/dot_general | solution.py:40
  (1 shorter events, 0.0 us)
Async XLA Ops:
  6.5 123.0 %all-gather.3.cloned.1.call-start = ((), (), s32[]{:S(2)}) async-start(), calls=%async_computation.2 | async-start | bytes 9216000 | tf_op jit(solution)/shard_map/all_gather | solution.py:20
  12.4 149.2 %all-to-all-start.1 = ((bf16[32,1280,80]{1,2,0:T(8,128)(2,1)}), bf16[32,1280,80]{1,2,0:T(8,128)(2,1)}, u32[]{:S(2)}, u32[]{:S(2)}) async-start(bf16[32,1280,80]{1,2,0:T(8,128)(2,1)} %broadcast_in_dim.2), calls=%async_computation.1 | async-start | bytes 13107200 | tf_op jit(solution)/shard_map/all_to_all | solution.py:16
  161.6 100.5 %all-to-all-start = ((f32[32,40,1280]{2,1,0:T(8,128)}), f32[32,40,1280]{2,1,0:T(8,128)}, u32[]{:S(2)}, u32[]{:S(2)}) async-start(f32[32,40,1280]{2,1,0:T(8,128)} %bitcast.11), calls=%async_computation | async-start | bytes 13107200 | tf_op jit(solution)/shard_map/all_to_all | solution.py:23
  171.2 174.5 %all-gather.5.cloned.1.call-start = ((), (), s32[]{:S(2)}) async-start(), calls=%async_computation.3 | async-start | bytes 2949120 | tf_op jit(solution)/shard_map/all_gather | solution.py:38
  171.2 174.5 %copy-start.1 = (f32[320,1280]{1,0:T(8,128)S(1)}, f32[320,1280]{1,0:T(8,128)}, u32[]{:S(2)}) copy-start(f32[320,1280]{1,0:T(8,128)} %param.7) | copy-start | bytes 4915204
  266.3 38.7 %collective-permute-start = (bf16[40,32,80]{2,1,0:T(8,128)(2,1)S(1)}, bf16[40,32,80]{2,1,0:T(8,128)(2,1)S(1)}, u32[]{:S(2)}, u32[]{:S(2)}) collective-permute-start(bf16[40,32,80]{2,1,0:T(8,128)(2,1)S(1)} %copy.9), channel_id=1, source_target_pairs={{0,0},{1,32},{2,64},{3,96},{4,128},{5,160},{6,192},{7,224},{8,1},{... | collective-permute-start | bytes 614408 | tf_op jit(solution)/shard_map/ppermute | solution.py:37
  304.9 0.7 copy-start
Sparse Core Ops, SparseCore 0:
  9.2 120.3 all-gather.2
  305.8 39.8 all-gather.4

commit v2 on v1

--- a/solution.py
+++ b/solution.py
@@ -34,8 +34,13 @@
     for w in range(n_wide):
         for n in range(n_narrow):
             perm.append((w * n_narrow + n, (n * blocks + w // n_narrow) * n_narrow + w % n_narrow))
-    left_piece = lax.ppermute(left_piece, ("wide", "narrow"), perm)
-    left_rows = lax.all_gather(left_piece, "narrow", axis=0, tiled=True)
+    arrived = []
+    for shift in range(n_narrow):
+        arrived.append(lax.ppermute(left_piece, ("wide", "narrow"), [
+            (src, (dst // n_narrow) * n_narrow + (dst % n_narrow + shift) % n_narrow) for src, dst in perm
+        ]))
+    order = (narrow_index - jnp.arange(n_narrow)) % n_narrow
+    left_rows = jnp.take(jnp.stack(arrived), order, axis=0).reshape((tile_rows,) + left_piece.shape[1:])
 
     update = lax.dot_general(
         left_rows, rc_all, (((1, 2), (0, 2)), ((), ())), preferred_element_type=jnp.float32

time: 364 us -> 439 us (1.21)
  starting transfers between devices: 20 us -> 55.8 us
  waiting for transfers between devices: 290 us -> 323 us
  local copies, waits for them, and re-layouts: 7.4 us -> 15.7 us
    ppermute x1 -> x8, waiting for transfers between devices: 36.7 us -> 110 us  [per_device(): lax.ppermute(left_piece, ('wide', 'narrow'), [(src, dst // n_narrow * n_n...]
    all_gather x1 -> x0, waiting for transfers between devices: 40 us -> none  [per_device(): left_rows = lax.all_gather(left_piece, 'narrow', axis=0, tiled=True)]
    ppermute x1 -> x8, starting transfers between devices: 1.92 us -> 37.8 us  [per_device(): lax.ppermute(left_piece, ('wide', 'narrow'), [(src, dst // n_narrow * n_n...]
    unnamed x5 -> x10, local copies, waits for them, and re-layouts: 0.89 us -> 5.67 us
  transfers between devices with their start and end apart: 5 -> 11, of which waited for: 5 -> 7; matrix products, arithmetic and copies ran while one was open for 7% -> 7% of each run, Pallas kernels for 0% -> 0%
where the time goes in v2:
time: 439 us
  waiting for transfers between devices  323 us (74%)
  starting transfers between devices  55.8 us (13%)
  matrix products  25.4 us (6%)
  local copies, waits for them, and re-layouts  15.7 us (4%)
  between operations  13.6 us (3%)
  other arithmetic  5.5 us (1%)
    ppermute x8, waiting for transfers between devices, per_device(): lax.ppermute(left_piece, ('wide', 'narrow'), [(src, dst // n_narrow * n_n...  110 us
    all_gather x1, waiting for transfers between devices, per_device(): cmm_full = lax.all_gather(cmm_panel, 'narrow', axis=1, tiled=True)  109 us
    all_to_all x1, waiting for transfers between devices, per_device(): lax.all_to_all(z_part.reshape(n_wide, piece, z_part.shape[1]), 'wide', 0,...  89.1 us
    ppermute x8, starting transfers between devices, per_device(): lax.ppermute(left_piece, ('wide', 'narrow'), [(src, dst // n_narrow * n_n...  37.8 us
    dot_general x1, matrix products, per_device(): z_part = jnp.dot(r_matrix, cmm_full, preferred_element_type=jnp.float32)  17.7 us
    all_to_all x1, waiting for transfers between devices, per_device(): lax.all_to_all(jnp.broadcast_to(rc[None], (n_wide,) + rc.shape), 'wide',...  14.3 us
    all_to_all x1, starting transfers between devices, per_device(): lax.all_to_all(z_part.reshape(n_wide, piece, z_part.shape[1]), 'wide', 0,...  9.54 us
  transfers between devices with their start and end apart: 11, of which 7 were waited for; matrix products, arithmetic and copies ran while one was open for 7% of the time, Pallas kernels for 0%

profile of v2, /device:TPU:42, one launch (start us, length us, event | category | flops | bytes accessed | tf_op | source)
XLA Modules:
  0.0 438.6 jit_solution(8337749811889363736)
XLA Ops:
  6.5 0.0 all-gather.2.cloned.1.call-start
  6.5 0.7 all-gather.2.cloned.1.call-update
  7.3 1.0 slice.9
  8.3 0.2 copy.20
  8.4 0.9 pad_maximum_fusion.1
  9.3 3.1 broadcast_in_dim.23
  12.4 8.5 %all-to-all-start.1 = ((bf16[32,1280,80]{1,2,0:T(8,128)(2,1)}), bf16[32,1280,80]{1,2,0:T(8,128)(2,1)}, u32[]{:S(2)}, u32[]{:S(2)}) async-start(bf16[32,1280,80]{1,2,0:T(8,128)(2,1)} %broadcast_in_dim.23), calls=%async_computation.1 | async-start | bytes 13107200 | tf_op jit(solution)/shard_map/all_to_all | solution.py:16
  20.9 108.7 %all-gather.2.cloned.1.call-done = bf16[3200,1280]{0,1:T(8,128)(2,1)} async-done(((bf16[3200,160]{0,1:T(8,128)(2,1)}), bf16[3200,1280]{0,1:T(8,128)(2,1)}) %all-gather.2.cloned.1.call-update) | async-done | bytes 8192016 | tf_op jit(solution)/shard_map/all_gather | solution.py:20
  129.5 17.7 %fusion.5 = f32[1280,1280]{1,0:T(8,128)} fusion(bf16[1280,3200]{1,0:T(8,128)(2,1)} %param.4, bf16[3200,1280]{0,1:T(8,128)(2,1)} %all-gather.2.cloned.1.call-done), kind=kOutput, calls=%fused_computation.31 | convolution fusion | flops 10485760000 | bytes 22937600 | tf_op jit(solution)/shard_map/dot_general | solution.py:21
  147.3 14.3 %all-to-all-done.1 = bf16[32,1280,80]{1,2,0:T(8,128)(2,1)} async-done(((bf16[32,1280,80]{1,2,0:T(8,128)(2,1)}), bf16[32,1280,80]{1,2,0:T(8,128)(2,1)}, u32[]{:S(2)}, u32[]{:S(2)}) %all-to-all-start.1) | async-done | bytes 6553632 | tf_op jit(solution)/shard_map/all_to_all | solution.py:16
  161.6 9.5 %all-to-all-start = ((f32[32,40,1280]{2,1,0:T(8,128)}), f32[32,40,1280]{2,1,0:T(8,128)}, u32[]{:S(2)}, u32[]{:S(2)}) async-start(f32[32,40,1280]{2,1,0:T(8,128)} %bitcast.31), calls=%async_computation | async-start | bytes 13107200 | tf_op jit(solution)/shard_map/all_to_all | solution.py:23
  171.2 0.1 broadcast_in_dim.20
  171.3 0.1 broadcast_in_dim.21
  171.4 1.6 dynamic-slice_bitcast_fusion
  173.0 89.1 %all-to-all-done = f32[32,40,1280]{2,1,0:T(8,128)} async-done(((f32[32,40,1280]{2,1,0:T(8,128)}), f32[32,40,1280]{2,1,0:T(8,128)}, u32[]{:S(2)}, u32[]{:S(2)}) %all-to-all-start) | async-done | bytes 6553632 | tf_op jit(solution)/shard_map/all_to_all | solution.py:23
  262.1 3.2 reduce_sum.9
  265.3 0.2 copy.9
  265.5 0.1 subtract_convert_fusion
  265.6 0.1 pad_maximum_fusion
  265.7 0.5 copy.11
  266.3 1.9 collective-permute-start
  268.2 16.0 %collective-permute-start.7 = (bf16[40,32,80]{2,1,0:T(8,128)(2,1)S(1)}, bf16[40,32,80]{2,1,0:T(8,128)(2,1)S(1)}, u32[]{:S(2)}, u32[]{:S(2)}) collective-permute-start(bf16[40,32,80]{2,1,0:T(8,128)(2,1)S(1)} %copy.11), channel_id=1, source_target_pairs={{0,7},{1,39},{2,71},{3,103},{4,135},{5,167},{6,199},{7,231},{8,0},... | collective-permute-start | bytes 614408 | tf_op jit(solution)/shard_map/ppermute | solution.py:39
  284.2 9.3 %collective-permute-start.6 = (bf16[40,32,80]{2,1,0:T(8,128)(2,1)S(1)}, bf16[40,32,80]{2,1,0:T(8,128)(2,1)S(1)}, u32[]{:S(2)}, u32[]{:S(2)}) collective-permute-start(bf16[40,32,80]{2,1,0:T(8,128)(2,1)S(1)} %copy.11), channel_id=1, source_target_pairs={{0,6},{1,38},{2,70},{3,102},{4,134},{5,166},{6,198},{7,230},{8,7},... | collective-permute-start | bytes 614408 | tf_op jit(solution)/shard_map/ppermute | solution.py:39
  293.5 1.9 collective-permute-start.5
  295.4 2.7 collective-permute-start.4
  298.2 37.3 %collective-permute-done = bf16[40,32,80]{2,1,0:T(8,128)(2,1)S(1)} collective-permute-done((bf16[40,32,80]{2,1,0:T(8,128)(2,1)S(1)}, bf16[40,32,80]{2,1,0:T(8,128)(2,1)S(1)}, u32[]{:S(2)}, u32[]{:S(2)}) %collective-permute-start) | collective-permute-done | bytes 204832 | tf_op jit(solution)/shard_map/ppermute | solution.py:39
  335.5 1.9 collective-permute-start.1
  337.4 0.7 bitcast_dynamic-update-slice_fusion.7
  338.2 22.3 %collective-permute-done.1 = bf16[40,32,80]{2,1,0:T(8,128)(2,1)S(1)} collective-permute-done((bf16[40,32,80]{2,1,0:T(8,128)(2,1)S(1)}, bf16[40,32,80]{2,1,0:T(8,128)(2,1)S(1)}, u32[]{:S(2)}, u32[]{:S(2)}) %collective-permute-start.1) | collective-permute-done | bytes 204832 | tf_op jit(solution)/shard_map/ppermute | solution.py:39
  360.4 1.9 collective-permute-start.2
  362.4 0.7 bitcast_dynamic-update-slice_fusion.6
  363.1 34.9 %collective-permute-done.2 = bf16[40,32,80]{2,1,0:T(8,128)(2,1)S(1)} collective-permute-done((bf16[40,32,80]{2,1,0:T(8,128)(2,1)S(1)}, bf16[40,32,80]{2,1,0:T(8,128)(2,1)S(1)}, u32[]{:S(2)}, u32[]{:S(2)}) %collective-permute-start.2) | collective-permute-done | bytes 204832 | tf_op jit(solution)/shard_map/ppermute | solution.py:39
  398.0 2.1 collective-permute-start.3
  400.1 0.7 bitcast_dynamic-update-slice_fusion.5
  400.9 15.3 %collective-permute-done.3 = bf16[40,32,80]{2,1,0:T(8,128)(2,1)S(1)} collective-permute-done((bf16[40,32,80]{2,1,0:T(8,128)(2,1)S(1)}, bf16[40,32,80]{2,1,0:T(8,128)(2,1)S(1)}, u32[]{:S(2)}, u32[]{:S(2)}) %collective-permute-start.3) | collective-permute-done | bytes 204832 | tf_op jit(solution)/shard_map/ppermute | solution.py:39
  416.1 0.8 bitcast_dynamic-update-slice_fusion.4
  416.9 0.0 collective-permute-done.4
  416.9 0.7 bitcast_dynamic-update-slice_fusion.3
  417.6 0.0 collective-permute-done.5
  417.6 0.7 bitcast_dynamic-update-slice_fusion.2
  418.4 0.0 collective-permute-done.6
  418.4 0.7 bitcast_dynamic-update-slice_fusion.1
  419.1 0.0 collective-permute-done.7
  419.1 0.7 bitcast_dynamic-update-slice_fusion
  419.9 2.8 gather_fusion
  422.7 0.0 copy-start
  422.7 1.1 bitcast_select_fusion
  423.8 0.3 copy-done
  424.1 7.6 %fusion = f32[320,1280]{1,0:T(8,128)} fusion(f32[320,1280]{1,0:T(8,128)S(1)} %copy-done, bf16[32,1280,80]{1,2,0:T(8,128)(2,1)} %all-to-all-done.1, bf16[320,32,80]{2,1,0:T(8,128)(2,1)S(1)} %bitcast_select_fusion), kind=kOutput, calls=%fused_computation.2 | convolution fusion | flops 2097561600 | bytes 11468800 | tf_op jit(solution)/shard_map/dot_general | solution.py:45
  (4 shorter events, 0.1 us)
Async XLA Ops:
  6.5 123.0 %all-gather.2.cloned.1.call-start = ((), (), s32[]{:S(2)}) async-start(), calls=%async_computation.2 | async-start | bytes 9216000 | tf_op jit(solution)/shard_map/all_gather | solution.py:20
  12.4 149.2 %all-to-all-start.1 = ((bf16[32,1280,80]{1,2,0:T(8,128)(2,1)}), bf16[32,1280,80]{1,2,0:T(8,128)(2,1)}, u32[]{:S(2)}, u32[]{:S(2)}) async-start(bf16[32,1280,80]{1,2,0:T(8,128)(2,1)} %broadcast_in_dim.23), calls=%async_computation.1 | async-start | bytes 13107200 | tf_op jit(solution)/shard_map/all_to_all | solution.py:16
  161.6 100.5 %all-to-all-start = ((f32[32,40,1280]{2,1,0:T(8,128)}), f32[32,40,1280]{2,1,0:T(8,128)}, u32[]{:S(2)}, u32[]{:S(2)}) async-start(f32[32,40,1280]{2,1,0:T(8,128)} %bitcast.31), calls=%async_computation | async-start | bytes 13107200 | tf_op jit(solution)/shard_map/all_to_all | solution.py:23
  266.3 69.3 %collective-permute-start = (bf16[40,32,80]{2,1,0:T(8,128)(2,1)S(1)}, bf16[40,32,80]{2,1,0:T(8,128)(2,1)S(1)}, u32[]{:S(2)}, u32[]{:S(2)}) collective-permute-start(bf16[40,32,80]{2,1,0:T(8,128)(2,1)S(1)} %copy.11), channel_id=1, source_target_pairs={{0,0},{1,32},{2,64},{3,96},{4,128},{5,160},{6,192},{7,224},{8,1},{... | collective-permute-start | bytes 614408 | tf_op jit(solution)/shard_map/ppermute | solution.py:39
  268.2 150.9 %collective-permute-start.7 = (bf16[40,32,80]{2,1,0:T(8,128)(2,1)S(1)}, bf16[40,32,80]{2,1,0:T(8,128)(2,1)S(1)}, u32[]{:S(2)}, u32[]{:S(2)}) collective-permute-start(bf16[40,32,80]{2,1,0:T(8,128)(2,1)S(1)} %copy.11), channel_id=1, source_target_pairs={{0,7},{1,39},{2,71},{3,103},{4,135},{5,167},{6,199},{7,231},{8,0},... | collective-permute-start | bytes 614408 | tf_op jit(solution)/shard_map/ppermute | solution.py:39
  284.2 134.1 %collective-permute-start.6 = (bf16[40,32,80]{2,1,0:T(8,128)(2,1)S(1)}, bf16[40,32,80]{2,1,0:T(8,128)(2,1)S(1)}, u32[]{:S(2)}, u32[]{:S(2)}) collective-permute-start(bf16[40,32,80]{2,1,0:T(8,128)(2,1)S(1)} %copy.11), channel_id=1, source_target_pairs={{0,6},{1,38},{2,70},{3,102},{4,134},{5,166},{6,198},{7,230},{8,7},... | collective-permute-start | bytes 614408 | tf_op jit(solution)/shard_map/ppermute | solution.py:39
  293.5 124.1 %collective-permute-start.5 = (bf16[40,32,80]{2,1,0:T(8,128)(2,1)S(1)}, bf16[40,32,80]{2,1,0:T(8,128)(2,1)S(1)}, u32[]{:S(2)}, u32[]{:S(2)}) collective-permute-start(bf16[40,32,80]{2,1,0:T(8,128)(2,1)S(1)} %copy.11), channel_id=1, source_target_pairs={{0,5},{1,37},{2,69},{3,101},{4,133},{5,165},{6,197},{7,229},{8,6},... | collective-permute-start | bytes 614408 | tf_op jit(solution)/shard_map/ppermute | solution.py:39
  295.4 121.5 %collective-permute-start.4 = (bf16[40,32,80]{2,1,0:T(8,128)(2,1)S(1)}, bf16[40,32,80]{2,1,0:T(8,128)(2,1)S(1)}, u32[]{:S(2)}, u32[]{:S(2)}) collective-permute-start(bf16[40,32,80]{2,1,0:T(8,128)(2,1)S(1)} %copy.11), channel_id=1, source_target_pairs={{0,4},{1,36},{2,68},{3,100},{4,132},{5,164},{6,196},{7,228},{8,5},... | collective-permute-start | bytes 614408 | tf_op jit(solution)/shard_map/ppermute | solution.py:39
  335.5 24.9 %collective-permute-start.1 = (bf16[40,32,80]{2,1,0:T(8,128)(2,1)S(1)}, bf16[40,32,80]{2,1,0:T(8,128)(2,1)S(1)}, u32[]{:S(2)}, u32[]{:S(2)}) collective-permute-start(bf16[40,32,80]{2,1,0:T(8,128)(2,1)S(1)} %copy.11), channel_id=1, source_target_pairs={{0,1},{1,33},{2,65},{3,97},{4,129},{5,161},{6,193},{7,225},{8,2},{... | collective-permute-start | bytes 614408 | tf_op jit(solution)/shard_map/ppermute | solution.py:39
  360.4 37.6 %collective-permute-start.2 = (bf16[40,32,80]{2,1,0:T(8,128)(2,1)S(1)}, bf16[40,32,80]{2,1,0:T(8,128)(2,1)S(1)}, u32[]{:S(2)}, u32[]{:S(2)}) collective-permute-start(bf16[40,32,80]{2,1,0:T(8,128)(2,1)S(1)} %copy.11), channel_id=1, source_target_pairs={{0,2},{1,34},{2,66},{3,98},{4,130},{5,162},{6,194},{7,226},{8,3},{... | collective-permute-start | bytes 614408 | tf_op jit(solution)/shard_map/ppermute | solution.py:39
  398.0 18.1 %collective-permute-start.3 = (bf16[40,32,80]{2,1,0:T(8,128)(2,1)S(1)}, bf16[40,32,80]{2,1,0:T(8,128)(2,1)S(1)}, u32[]{:S(2)}, u32[]{:S(2)}) collective-permute-start(bf16[40,32,80]{2,1,0:T(8,128)(2,1)S(1)} %copy.11), channel_id=1, source_target_pairs={{0,3},{1,35},{2,67},{3,99},{4,131},{5,163},{6,195},{7,227},{8,4},{... | collective-permute-start | bytes 614408 | tf_op jit(solution)/shard_map/ppermute | solution.py:39
  422.7 1.4 copy-start
Sparse Core Ops, SparseCore 0:
  9.2 120.3 all-gather.1

commit v3 on v1

v3 whole, which is shorter than its diff:
```python
import jax
import jax.numpy as jnp
from jax import lax
from jax.sharding import PartitionSpec as P

N_CHUNKS = 2


def per_device(r_matrix, cmm_panel, ctm_panel, cee_in, n_wide, n_narrow):
    slope_rows = r_matrix.shape[0]
    tile_rows = cee_in.shape[0]
    panel_width = ctm_panel.shape[1]
    cols = cmm_panel.shape[1]
    width = cols // N_CHUNKS
    piece = slope_rows // n_wide
    wide_index = lax.axis_index("wide")

    rc = jnp.concatenate([r_matrix[:, :panel_width], ctm_panel], axis=1)
    rc_all = lax.all_to_all(
        jnp.broadcast_to(rc[None], (n_wide,) + rc.shape), "wide", 0, 0, tiled=True
    )

    blocks = n_wide // n_narrow
    perm = []
    for w in range(n_wide):
        for n in range(n_narrow):
            perm.append((w * n_narrow + n, (n * blocks + w // n_narrow) * n_narrow + w % n_narrow))

    rc_rows = lax.all_to_all(rc.reshape(n_wide, piece, rc.shape[1]), "wide", 0, 0, tiled=True)
    rc_rows = jnp.transpose(rc_rows, (1, 0, 2))
    ctm_rows = rc_rows[:, :, panel_width:].astype(jnp.float32).reshape(
        piece, n_narrow, N_CHUNKS, width // panel_width, panel_width
    )
    r_rows = rc_rows[:, :, :panel_width].reshape(piece, n_wide * panel_width)

    zw = n_narrow * width
    left = []
    cmm_next = cmm_panel[:, :width]
    for chunk in range(N_CHUNKS):
        cmm_c = lax.all_gather(cmm_next, "narrow", axis=1, tiled=True)
        z_c = jnp.dot(r_matrix, cmm_c, preferred_element_type=jnp.float32)
        if chunk + 1 < N_CHUNKS:
            cmm_next, z_c = lax.optimization_barrier(
                (cmm_panel[:, (chunk + 1) * width:(chunk + 2) * width], z_c)
            )
        else:
            rc_all, z_c = lax.optimization_barrier((rc_all, z_c))
        recv = lax.all_to_all(
            z_c.reshape(n_wide, piece, zw), "wide", 0, 0, tiled=True
        )
        z_sum = jnp.sum(recv, axis=0).reshape(piece, n_narrow, width // panel_width, panel_width)
        a_c = (z_sum - ctm_rows[:, :, chunk]).astype(jnp.bfloat16).reshape(piece, zw)
        if chunk == 0:
            a_c = jnp.concatenate([a_c, r_rows], axis=1)
        a_c = lax.ppermute(a_c, ("wide", "narrow"), perm)
        left.append(lax.all_gather(a_c, "narrow", axis=0, tiled=True))

    rc5 = rc_all.reshape(n_narrow, N_CHUNKS, width // panel_width, slope_rows, 2 * panel_width)
    update = None
    for chunk in range(N_CHUNKS):
        a_rows = left[chunk][:, :n_narrow * width].reshape(
            tile_rows, n_narrow, width // panel_width, panel_width
        )
        term = lax.dot_general(
            a_rows, rc5[:, chunk, :, :, :panel_width], (((1, 2, 3), (0, 1, 3)), ((), ())),
            preferred_element_type=jnp.float32,
        )
        update = term if update is None else update + term
    r_rows = left[0][:, n_narrow * width:].reshape(tile_rows, n_wide, panel_width)
    update = update - lax.dot_general(
        r_rows, rc_all[:, :, panel_width:], (((1, 2), (0, 2)), ((), ())),
        preferred_element_type=jnp.float32,
    )
    return cee_in + update


def solution(mesh):
    n_wide, n_narrow = mesh.shape["wide"], mesh.shape["narrow"]
    placed = (P("narrow", "wide"), P("wide", "narrow"), P("narrow", "wide"), P("wide", "narrow"))

    def body(r_matrix, cmm_panel, ctm_panel, cee_in):
        return per_device(r_matrix, cmm_panel, ctm_panel, cee_in, n_wide, n_narrow)

    return jax.shard_map(
        body, mesh=mesh, in_specs=placed, out_specs=P("wide", "narrow"), check_vma=False
    )
```

time: 364 us -> 379 us (1.041)
  waiting for transfers between devices: 290 us -> 218 us
  starting transfers between devices: 20 us -> 50.9 us
  local copies, waits for them, and re-layouts: 7.4 us -> 34.3 us
  blocking collectives: 0 us -> 18.2 us
  matrix products: 26.2 us -> 35.5 us
    all_to_all x1 -> x3, waiting for transfers between devices: 89.1 us -> 24.8 us  [the longest x2 18.8 us: per_device(): lax.all_to_all(z_c.reshape(n_wide, piece, zw), 'wide', 0, 0, tiled=True)]
    all_to_all x1, waiting for transfers between devices: 14.3 us -> 53.5 us  [per_device(): lax.all_to_all(jnp.broadcast_to(rc[None], (n_wide,) + rc.shape), 'wide',...]
    all_to_all x1 -> x3, starting transfers between devices: 9.54 us -> 38.9 us  [the longest x2 30.5 us: per_device(): lax.all_to_all(z_c.reshape(n_wide, piece, zw), 'wide', 0, 0, tiled=True)]
    all_gather x2 -> x3, waiting for transfers between devices: 149 us -> 120 us  [the longest x2 70.8 us: per_device(): cmm_c = lax.all_gather(cmm_next, 'narrow', axis=1, tiled=True)]
    all_gather x0 -> x1, blocking collectives: none -> 18.2 us  [per_device(): left.append(lax.all_gather(a_c, 'narrow', axis=0, tiled=True))]
    ppermute x1 -> x2, waiting for transfers between devices: 36.7 us -> 19.4 us  [per_device(): a_c = lax.ppermute(a_c, ('wide', 'narrow'), perm)]
    slice x0 -> x9, local copies, waits for them, and re-layouts: none -> 14.5 us  [the longest x2 4.29 us: per_device(): left[0][:, n_narrow * width:].reshape(tile_rows, n_wide, panel_width)]
    dot_general x2 -> x5, matrix products: 26.2 us -> 35.5 us  [the longest x2 22.7 us: per_device(): z_c = jnp.dot(r_matrix, cmm_c, preferred_element_type=jnp.float32)]
  transfers between devices with their start and end apart: 5 -> 9, of which waited for: 5 -> 7; matrix products, arithmetic and copies ran while one was open for 7% -> 16% of each run, Pallas kernels for 0% -> 0%
where the time goes in v3:
time: 379 us; the launch traced here: 375 us
  waiting for transfers between devices  218 us (58%)
  starting transfers between devices  50.9 us (13%)
  matrix products  35.5 us (9%)
  local copies, waits for them, and re-layouts  34.3 us (9%)
  blocking collectives  18.2 us (5%)
  between operations  13.2 us (3%)
  other arithmetic  4.75 us (1%)
    all_gather x2, waiting for transfers between devices, per_device(): cmm_c = lax.all_gather(cmm_next, 'narrow', axis=1, tiled=True)  70.8 us
    all_to_all x1, waiting for transfers between devices, per_device(): lax.all_to_all(jnp.broadcast_to(rc[None], (n_wide,) + rc.shape), 'wide',...  53.5 us
    all_gather x1, waiting for transfers between devices, per_device(): left.append(lax.all_gather(a_c, 'narrow', axis=0, tiled=True))  49.6 us
    all_to_all x2, starting transfers between devices, per_device(): lax.all_to_all(z_c.reshape(n_wide, piece, zw), 'wide', 0, 0, tiled=True)  30.5 us
    dot_general x2, matrix products, per_device(): z_c = jnp.dot(r_matrix, cmm_c, preferred_element_type=jnp.float32)  22.7 us
    ppermute x2, waiting for transfers between devices, per_device(): a_c = lax.ppermute(a_c, ('wide', 'narrow'), perm)  19.4 us
    all_to_all x2, waiting for transfers between devices, per_device(): lax.all_to_all(z_c.reshape(n_wide, piece, zw), 'wide', 0, 0, tiled=True)  18.8 us
    all_gather x1, blocking collectives, per_device(): left.append(lax.all_gather(a_c, 'narrow', axis=0, tiled=True))  18.2 us
  transfers between devices with their start and end apart: 9, of which 7 were waited for; matrix products, arithmetic and copies ran while one was open for 16% of the time, Pallas kernels for 0%

profile of v3, /device:TPU:42, one launch (start us, length us, event | category | flops | bytes accessed | tf_op | source)
XLA Modules:
  0.0 374.9 jit_solution(15256736422750464481)
XLA Ops:
  6.5 1.1 copy.26
  7.6 1.0 slice.38
  8.7 0.9 pad_maximum_fusion
  9.6 8.4 %all-to-all-start.1 = ((bf16[32,40,80]{2,1,0:T(8,128)(2,1)}), bf16[32,40,80]{2,1,0:T(8,128)(2,1)S(1)}, u32[]{:S(2)}, u32[]{:S(2)}) async-start(bf16[32,40,80]{2,1,0:T(8,128)(2,1)} %bitcast.1), calls=%async_computation.1 | async-start | bytes 655360 | tf_op jit(solution)/shard_map/all_to_all | solution.py:29
  18.0 1.2 copy.30
  19.1 6.0 %all-to-all-done.1 = bf16[32,40,80]{2,1,0:T(8,128)(2,1)S(1)} async-done(((bf16[32,40,80]{2,1,0:T(8,128)(2,1)}), bf16[32,40,80]{2,1,0:T(8,128)(2,1)S(1)}, u32[]{:S(2)}, u32[]{:S(2)}) %all-to-all-start.1) | async-done | bytes 204832 | tf_op jit(solution)/shard_map/all_to_all | solution.py:29
  25.1 0.0 copy-start.1
  25.1 3.2 broadcast_in_dim.2
  28.3 0.0 copy-done.1
  28.3 0.0 copy-start.2
  28.3 8.0 %all-to-all-start.2 = ((bf16[32,1280,80]{1,2,0:T(8,128)(2,1)}), bf16[32,1280,80]{1,2,0:T(8,128)(2,1)}, u32[]{:S(2)}, u32[]{:S(2)}) async-start(bf16[32,1280,80]{1,2,0:T(8,128)(2,1)} %broadcast_in_dim.2), calls=%async_computation.2 | async-start | bytes 13107200 | tf_op jit(solution)/shard_map/all_to_all | solution.py:19
  36.3 0.0 all-gather.4.cloned.1.call-start
  36.4 0.0 copy-done.2
  36.4 1.0 fusion.8
  37.4 0.0 all-gather.4.cloned.1.call-update
  37.4 0.0 all-gather.8.cloned.1.call-start
  37.5 70.7 %all-gather.4.cloned.1.call-done = bf16[3200,640]{0,1:T(8,128)(2,1)} async-done(((bf16[3200,80]{0,1:T(8,128)(2,1)}), bf16[3200,640]{0,1:T(8,128)(2,1)}) %all-gather.4.cloned.1.call-update) | async-done | bytes 4096016 | tf_op jit(solution)/shard_map/all_gather | solution.py:40
  108.2 11.5 %fusion.11 = f32[1280,640]{1,0:T(8,128)} fusion(bf16[1280,3200]{1,0:T(8,128)(2,1)} %param.4, bf16[3200,640]{0,1:T(8,128)(2,1)} %all-gather.4.cloned.1.call-done), kind=kOutput, calls=%fused_computation.18 | convolution fusion | flops 5242880000 | bytes 15564800 | tf_op jit(solution)/shard_map/dot_general | solution.py:41
  119.7 0.0 all-gather.8.cloned.1.call-update
  119.7 53.5 %all-to-all-done.2 = bf16[32,1280,80]{1,2,0:T(8,128)(2,1)} async-done(((bf16[32,1280,80]{1,2,0:T(8,128)(2,1)}), bf16[32,1280,80]{1,2,0:T(8,128)(2,1)}, u32[]{:S(2)}, u32[]{:S(2)}) %all-to-all-start.2) | async-done | bytes 6553632 | tf_op jit(solution)/shard_map/all_to_all | solution.py:19
  173.3 17.7 %all-to-all-start = ((f32[32,40,640]{2,1,0:T(8,128)}), f32[32,40,640]{2,1,0:T(8,128)S(1)}, u32[]{:S(2)}, u32[]{:S(2)}) async-start(f32[32,40,640]{2,1,0:T(8,128)} %bitcast.49), calls=%async_computation | async-start | bytes 6553600 | tf_op jit(solution)/shard_map/all_to_all | solution.py:48
  191.0 0.0 all-gather.8.cloned.1.call-done
  191.0 11.1 %convolution_bitcast_fusion = f32[1280,640]{0,1:T(8,128)} fusion(bf16[3200,640]{0,1:T(8,128)(2,1)} %all-gather.8.cloned.1.call-done, bf16[1280,3200]{1,0:T(8,128)(2,1)} %param.4), kind=kOutput, calls=%fused_computation | convolution fusion | flops 5242880000 | bytes 15564800 | tf_op jit(solution)/shard_map/dot_general | solution.py:41
  202.1 4.6 %copy.32 = f32[1280,640]{1,0:T(8,128)} copy(f32[1280,640]{0,1:T(8,128)} %convolution_bitcast_fusion) | data formatting | bytes 6553600 | tf_op jit(solution)/shard_map/optimization_barrier | solution.py:47
  206.7 18.8 %all-to-all-done = f32[32,40,640]{2,1,0:T(8,128)S(1)} async-done(((f32[32,40,640]{2,1,0:T(8,128)}), f32[32,40,640]{2,1,0:T(8,128)S(1)}, u32[]{:S(2)}, u32[]{:S(2)}) %all-to-all-start) | async-done | bytes 3276832 | tf_op jit(solution)/shard_map/all_to_all | solution.py:48
  225.5 0.0 copy-start
  225.5 1.8 copy-done
  227.2 12.8 %all-to-all-start.3 = ((f32[32,40,640]{2,1,0:T(8,128)}), f32[32,40,640]{2,1,0:T(8,128)S(1)}, u32[]{:S(2)}, u32[]{:S(2)}) async-start(f32[32,40,640]{2,1,0:T(8,128)} %bitcast.10), calls=%async_computation.3 | async-start | bytes 6553600 | tf_op jit(solution)/shard_map/all_to_all | solution.py:48
  240.1 0.0 all-gather.6.cloned.1.call-start
  240.1 2.0 fusion.10
  242.1 0.8 copy.28
  242.8 1.4 reshape.41
  244.2 1.8 fusion.9
  246.0 0.9 copy.27
  246.9 1.4 squeeze.12
  248.3 2.7 reduce_sum.18
  251.0 0.9 subtract_convert_fusion.1
  252.0 1.9 collective-permute-start
  253.9 15.8 %collective-permute-done = bf16[40,1920]{1,0:T(8,128)(2,1)S(1)} collective-permute-done((bf16[40,1920]{1,0:T(8,128)(2,1)S(1)}, bf16[40,1920]{1,0:T(8,128)(2,1)S(1)}, u32[]{:S(2)}, u32[]{:S(2)}) %collective-permute-start) | collective-permute-done | bytes 153632 | tf_op jit(solution)/shard_map/ppermute | solution.py:55
  269.7 0.0 copy-start.3
  269.7 0.7 copy-done.3
  270.4 0.0 all-gather.6.cloned.1.call-update
  270.4 1.9 copy.40
  272.2 1.4 squeeze.14
  273.6 49.6 %all-gather.6.cloned.1.call-done = bf16[320,1920]{1,0:T(8,128)(2,1)} async-done(((bf16[40,1920]{1,0:T(8,128)(2,1)}), bf16[320,1920]{1,0:T(8,128)(2,1)}) %all-gather.6.cloned.1.call-update) | async-done | bytes 1228816 | tf_op jit(solution)/shard_map/all_gather | solution.py:56
  323.2 2.1 slice.55
  325.3 2.2 copy.36
  327.5 1.8 slice.51
  329.3 2.0 copy.29
  331.3 4.7 %fusion.5 = f32[320,1280]{1,0:T(8,128)} fusion(bf16[320,32,40]{0,2,1:T(8,128)(2,1)} %bitcast.52, bf16[32,1280,80]{1,2,0:T(8,128)(2,1)} %all-to-all-done.2), kind=kOutput, calls=%fused_computation.8 | convolution fusion | flops 1048576000 | bytes 5898240 | tf_op jit(solution)/shard_map/dot_general | solution.py:70
  336.0 0.0 all-to-all-done.3
  336.0 0.2 reduce_sum.19
  336.2 2.0 collective-permute-start.1
  338.1 0.0 copy-start.4
  338.1 3.7 convolution_bitcast_fusion.2
  341.9 3.6 collective-permute-done.1
  345.5 18.2 %all_gather.15 = bf16[320,640]{1,0:T(8,128)(2,1)S(1)} all-gather(bf16[40,640]{1,0:T(8,128)(2,1)S(1)} %collective-permute-done.1), channel_id=1, replica_groups=mesh['wide'=32,'narrow'=8] {'narrow'}, dimensions={0}, use_global_device_ids=true | all-gather | bytes 460800 | tf_op jit(solution)/shard_map/all_gather | solution.py:56
  363.7 0.3 copy.34
  363.9 0.0 copy-done.4
  363.9 4.4 %fusion.4 = f32[320,1280]{1,0:T(8,128)} fusion(f32[320,1280]{1,0:T(8,128)S(1)} %copy-done.4, f32[320,1280]{1,0:T(8,128)} %fusion.5, f32[320,1280]{1,0:T(8,128)} %convolution_bitcast_fusion.2, bf16[320,8,2,40]{0,3,2,1:T(8,128)(2,1)S(1)} %bitcast.54, bf16[8,2,2,1280,80]{3,4,2,1,0:T(8,128)(2,1)} %bitcast.6), kind=kOutput, calls=%fused_computation.6 | convolution fusion | flops 525516800 | bytes 8601600 | tf_op jit(solution)/shard_map/dot_general | solution.py:64
  (2 shorter events, 0.0 us)
Async XLA Ops:
  9.6 15.6 %all-to-all-start.1 = ((bf16[32,40,80]{2,1,0:T(8,128)(2,1)}), bf16[32,40,80]{2,1,0:T(8,128)(2,1)S(1)}, u32[]{:S(2)}, u32[]{:S(2)}) async-start(bf16[32,40,80]{2,1,0:T(8,128)(2,1)} %bitcast.1), calls=%async_computation.1 | async-start | bytes 655360 | tf_op jit(solution)/shard_map/all_to_all | solution.py:29
  25.1 3.2 copy-start.1
  28.3 8.0 %copy-start.2 = (bf16[3200,160]{0,1:T(8,128)(2,1)S(1)}, bf16[3200,160]{0,1:T(8,128)(2,1)}, u32[]{:S(2)}) copy-start(bf16[3200,160]{0,1:T(8,128)(2,1)} %param.5) | copy-start | bytes 3072004
  28.3 144.9 %all-to-all-start.2 = ((bf16[32,1280,80]{1,2,0:T(8,128)(2,1)}), bf16[32,1280,80]{1,2,0:T(8,128)(2,1)}, u32[]{:S(2)}, u32[]{:S(2)}) async-start(bf16[32,1280,80]{1,2,0:T(8,128)(2,1)} %broadcast_in_dim.2), calls=%async_computation.2 | async-start | bytes 13107200 | tf_op jit(solution)/shard_map/all_to_all | solution.py:19
  36.3 71.9 %all-gather.4.cloned.1.call-start = ((), (), s32[]{:S(2)}) async-start(), calls=%async_computation.4 | async-start | bytes 4608000 | tf_op jit(solution)/shard_map/all_gather | solution.py:40
  37.4 153.6 %all-gather.8.cloned.1.call-start = ((), (), s32[]{:S(2)}) async-start(), calls=%async_computation.6 | async-start | bytes 4608000 | tf_op jit(solution)/shard_map/all_gather | solution.py:40
  173.3 52.2 %all-to-all-start = ((f32[32,40,640]{2,1,0:T(8,128)}), f32[32,40,640]{2,1,0:T(8,128)S(1)}, u32[]{:S(2)}, u32[]{:S(2)}) async-start(f32[32,40,640]{2,1,0:T(8,128)} %bitcast.49), calls=%async_computation | async-start | bytes 6553600 | tf_op jit(solution)/shard_map/all_to_all | solution.py:48
  225.5 1.8 copy-start
  227.2 108.7 %all-to-all-start.3 = ((f32[32,40,640]{2,1,0:T(8,128)}), f32[32,40,640]{2,1,0:T(8,128)S(1)}, u32[]{:S(2)}, u32[]{:S(2)}) async-start(f32[32,40,640]{2,1,0:T(8,128)} %bitcast.10), calls=%async_computation.3 | async-start | bytes 6553600 | tf_op jit(solution)/shard_map/all_to_all | solution.py:48
  240.1 83.2 %all-gather.6.cloned.1.call-start = ((), (), s32[]{:S(2)}) async-start(), calls=%async_computation.5 | async-start | bytes 1382400 | tf_op jit(solution)/shard_map/all_gather | solution.py:56
  252.0 17.7 %collective-permute-start = (bf16[40,1920]{1,0:T(8,128)(2,1)S(1)}, bf16[40,1920]{1,0:T(8,128)(2,1)S(1)}, u32[]{:S(2)}, u32[]{:S(2)}) collective-permute-start(bf16[40,1920]{1,0:T(8,128)(2,1)S(1)} %pad_maximum_fusion.1), channel_id=1, source_target_pairs={{0,0},{1,32},{2,64},{3,96},{4,128},{5,160},{6,192},{7,224},{8,1},{... | collective-permute-start | bytes 460808 | tf_op jit(solution)/shard_map/ppermute | solution.py:55
  269.7 0.7 copy-start.3
  336.2 9.3 %collective-permute-start.1 = (bf16[40,640]{1,0:T(8,128)(2,1)S(1)}, bf16[40,640]{1,0:T(8,128)(2,1)S(1)}, u32[]{:S(2)}, u32[]{:S(2)}) collective-permute-start(bf16[40,640]{1,0:T(8,128)(2,1)S(1)} %subtract_convert_fusion), channel_id=1, source_target_pairs={{0,0},{1,32},{2,64},{3,96},{4,128},{5,160},{6,192},{7,224},{8,1},{... | collective-permute-start | bytes 153608 | tf_op jit(solution)/shard_map/ppermute | solution.py:55
  338.1 25.8 %copy-start.4 = (f32[320,1280]{1,0:T(8,128)S(1)}, f32[320,1280]{1,0:T(8,128)}, u32[]{:S(2)}) copy-start(f32[320,1280]{1,0:T(8,128)} %param.7) | copy-start | bytes 4915204
Sparse Core Ops, SparseCore 0:
  39.0 69.2 all-gather.3
  119.9 63.2 all-gather.7
  270.5 52.6 all-gather.5

commit v4 on v1

--- a/solution.py
+++ b/solution.py
@@ -13,21 +13,24 @@
     narrow_index = lax.axis_index("narrow")
 
     rc = jnp.concatenate([r_matrix[:, :panel_width], ctm_panel], axis=1)
-    rc_all = lax.all_to_all(
-        jnp.broadcast_to(rc[None], (n_wide,) + rc.shape), "wide", 0, 0, tiled=True
-    )
 
     cmm_full = lax.all_gather(cmm_panel, "narrow", axis=1, tiled=True)
     z_part = jnp.dot(r_matrix, cmm_full, preferred_element_type=jnp.float32)
+    z_part = jnp.concatenate([z_part, rc.astype(jnp.float32)], axis=1)
 
     z_recv = lax.all_to_all(
         z_part.reshape(n_wide, piece, z_part.shape[1]), "wide", 0, 0, tiled=True
     )
-    z_mine = jnp.sum(z_recv, axis=0).reshape(piece, n_wide, panel_width)
-    rc_rows = lax.dynamic_slice_in_dim(rc_all, wide_index * piece, piece, 1)
-    rc_rows = jnp.transpose(rc_rows, (1, 0, 2))
-    a_piece = (z_mine - rc_rows[:, :, panel_width:].astype(jnp.float32)).astype(jnp.bfloat16)
-    left_piece = jnp.concatenate([a_piece, -rc_rows[:, :, :panel_width]], axis=2)
+    n_cols = n_wide * panel_width
+    z_mine = jnp.sum(z_recv[:, :, :n_cols], axis=0).reshape(piece, n_wide, panel_width)
+    rc_rows = jnp.transpose(z_recv[:, :, n_cols:], (1, 0, 2))
+    a_piece = (z_mine - rc_rows[:, :, panel_width:]).astype(jnp.bfloat16)
+    left_piece = jnp.concatenate([a_piece, -rc_rows[:, :, :panel_width].astype(jnp.bfloat16)], axis=2)
+
+    rc, z_recv = lax.optimization_barrier((rc, z_recv))
+    rc_all = lax.all_to_all(
+        jnp.broadcast_to(rc[None], (n_wide,) + rc.shape), "wide", 0, 0, tiled=True
+    )
 
     blocks = n_wide // n_narrow
     perm = []

time: 364 us -> 407 us (1.12)
  blocking collectives: 0 us -> 90.1 us
  waiting for transfers between devices: 290 us -> 244 us
  starting transfers between devices: 20 us -> 10.8 us
  local copies, waits for them, and re-layouts: 7.4 us -> 15.1 us
    all_to_all x0 -> x1, blocking collectives: none -> 90.1 us  [per_device(): lax.all_to_all(z_part.reshape(n_wide, piece, z_part.shape[1]), 'wide', 0,...]
    all_to_all x1 -> x0, waiting for transfers between devices: 89.1 us -> none  [per_device(): lax.all_to_all(z_part.reshape(n_wide, piece, z_part.shape[1]), 'wide', 0,...]
    all_gather x1, waiting for transfers between devices: 40 us -> 128 us  [per_device(): left_rows = lax.all_gather(left_piece, 'narrow', axis=0, tiled=True)]
    all_gather x1, waiting for transfers between devices: 109 us -> 87.7 us  [per_device(): cmm_full = lax.all_gather(cmm_panel, 'narrow', axis=1, tiled=True)]
    all_to_all x1, waiting for transfers between devices: 14.3 us -> 0.01 us  [per_device(): lax.all_to_all(jnp.broadcast_to(rc[None], (n_wide,) + rc.shape), 'wide',...]
    all_to_all x1 -> x0, starting transfers between devices: 9.54 us -> none  [per_device(): lax.all_to_all(z_part.reshape(n_wide, piece, z_part.shape[1]), 'wide', 0,...]
    ppermute x1, waiting for transfers between devices: 36.7 us -> 27.6 us  [per_device(): left_piece = lax.ppermute(left_piece, ('wide', 'narrow'), perm)]
    concatenate x1, local copies, waits for them, and re-layouts: 0.51 us -> 8.54 us  [per_device(): z_part = jnp.concatenate([z_part, rc.astype(jnp.float32)], axis=1)]
  transfers between devices with their start and end apart: 5 -> 4, of which waited for: 5 -> 3; matrix products, arithmetic and copies ran while one was open for 7% -> 2% of each run, Pallas kernels for 0% -> 0%
where the time goes in v4:
time: 407 us; the launch traced here: 405 us
  waiting for transfers between devices  244 us (60%)
  blocking collectives  90.1 us (22%)
  matrix products  23.5 us (6%)
  local copies, waits for them, and re-layouts  15.1 us (4%)
  between operations  13.5 us (3%)
  starting transfers between devices  10.8 us (3%)
  other arithmetic  8.24 us (2%)
    all_gather x1, waiting for transfers between devices, per_device(): left_rows = lax.all_gather(left_piece, 'narrow', axis=0, tiled=True)  128 us
    all_to_all x1, blocking collectives, per_device(): lax.all_to_all(z_part.reshape(n_wide, piece, z_part.shape[1]), 'wide', 0,...  90.1 us
    all_gather x1, waiting for transfers between devices, per_device(): cmm_full = lax.all_gather(cmm_panel, 'narrow', axis=1, tiled=True)  87.7 us
    ppermute x1, waiting for transfers between devices, per_device(): left_piece = lax.ppermute(left_piece, ('wide', 'narrow'), perm)  27.6 us
    dot_general x1, matrix products, per_device(): z_part = jnp.dot(r_matrix, cmm_full, preferred_element_type=jnp.float32)  16 us
    all_to_all x1, starting transfers between devices, per_device(): lax.all_to_all(jnp.broadcast_to(rc[None], (n_wide,) + rc.shape), 'wide',...  8.8 us
    concatenate x1, local copies, waits for them, and re-layouts, per_device(): z_part = jnp.concatenate([z_part, rc.astype(jnp.float32)], axis=1)  8.54 us
  transfers between devices with their start and end apart: 4, of which 3 were waited for; matrix products, arithmetic and copies ran while one was open for 2% of the time, Pallas kernels for 0%

profile of v4, /device:TPU:42, one launch (start us, length us, event | category | flops | bytes accessed | tf_op | source)
XLA Modules:
  0.0 404.8 jit_solution(1084379023431749944)
XLA Ops:
  6.5 0.0 all-gather.3.cloned.1.call-start
  6.5 0.7 all-gather.3.cloned.1.call-update
  7.3 1.0 slice.16
  8.3 0.2 copy.10
  8.4 0.9 pad_maximum_fusion.2
  9.4 87.7 %all-gather.3.cloned.1.call-done = bf16[3200,1280]{0,1:T(8,128)(2,1)} async-done(((bf16[3200,160]{0,1:T(8,128)(2,1)}), bf16[3200,1280]{0,1:T(8,128)(2,1)}) %all-gather.3.cloned.1.call-update) | async-done | bytes 8192016 | tf_op jit(solution)/shard_map/all_gather | solution.py:17
  97.1 16.0 %fusion.4 = f32[1280,1280]{0,1:T(8,128)S(1)} fusion(bf16[1280,3200]{1,0:T(8,128)(2,1)} %param.4, bf16[3200,1280]{0,1:T(8,128)(2,1)} %all-gather.3.cloned.1.call-done), kind=kOutput, calls=%fused_computation.12 | convolution fusion | flops 10485760000 | bytes 22937600 | tf_op jit(solution)/shard_map/dot_general | solution.py:18
  113.1 3.3 pad_maximum_fusion
  116.4 8.5 %copy.8 = f32[1280,1360]{1,0:T(8,128)} copy(f32[1280,1360]{0,1:T(8,128)} %pad_maximum_fusion) | data formatting | bytes 13926400 | tf_op jit(solution)/shard_map/concatenate | solution.py:19
  125.0 90.1 %all_to_all.10 = f32[32,40,1360]{2,1,0:T(8,128)} all-to-all(f32[32,40,1360]{2,1,0:T(8,128)} %bitcast.11), channel_id=1, replica_groups=mesh['wide'=32,'narrow'=8] {'wide'}, dimensions={0} | all-to-all | bytes 13926400 | tf_op jit(solution)/shard_map/all_to_all | solution.py:21
  215.0 3.1 broadcast_in_dim.2
  218.1 8.8 %all-to-all-start.1 = ((bf16[32,1280,80]{1,2,0:T(8,128)(2,1)}), bf16[32,1280,80]{1,2,0:T(8,128)(2,1)}, u32[]{:S(2)}, u32[]{:S(2)}) async-start(bf16[32,1280,80]{1,2,0:T(8,128)(2,1)} %broadcast_in_dim.2), calls=%async_computation.1 | async-start | bytes 13107200 | tf_op jit(solution)/shard_map/all_to_all | solution.py:31
  226.9 0.0 copy-start.1
  226.9 0.0 all-gather.5.cloned.1.call-start
  227.0 3.3 slice_reduce_fusion
  230.3 0.5 reshape.8
  230.8 1.1 slice_bitcast_fusion
  231.9 0.1 fusion.2
  232.0 0.4 fusion.1
  232.4 0.2 pad_maximum_fusion.1
  232.6 1.9 collective-permute-start
  234.5 27.6 %collective-permute-done = bf16[40,32,80]{2,0,1:T(8,128)(2,1)S(1)} collective-permute-done((bf16[40,32,80]{2,0,1:T(8,128)(2,1)S(1)}, bf16[40,32,80]{2,0,1:T(8,128)(2,1)S(1)}, u32[]{:S(2)}, u32[]{:S(2)}) %collective-permute-start) | collective-permute-done | bytes 204832 | tf_op jit(solution)/shard_map/ppermute | solution.py:40
  262.1 0.0 copy-start
  262.1 0.7 copy-done
  262.8 0.0 all-gather.5.cloned.1.call-update
  262.9 127.6 %all-gather.5.cloned.1.call-done = bf16[320,32,80]{2,0,1:T(8,128)(2,1)} async-done(((bf16[40,32,80]{2,0,1:T(8,128)(2,1)}), bf16[320,32,80]{2,0,1:T(8,128)(2,1)}) %all-gather.5.cloned.1.call-update) | async-done | bytes 1638416 | tf_op jit(solution)/shard_map/all_gather | solution.py:41
  390.5 0.0 all-to-all-done.1
  390.5 0.0 copy-done.1
  390.5 7.5 %fusion = f32[320,1280]{1,0:T(8,128)} fusion(f32[320,1280]{1,0:T(8,128)S(1)} %copy-done.1, bf16[320,32,80]{2,0,1:T(8,128)(2,1)} %all-gather.5.cloned.1.call-done, bf16[32,1280,80]{1,2,0:T(8,128)(2,1)} %all-to-all-done.1), kind=kOutput, calls=%fused_computation.3 | convolution fusion | flops 2097561600 | bytes 11468800 | tf_op jit(solution)/shard_map/dot_general | solution.py:43
Async XLA Ops:
  6.5 90.5 %all-gather.3.cloned.1.call-start = ((), (), s32[]{:S(2)}) async-start(), calls=%async_computation.2 | async-start | bytes 9216000 | tf_op jit(solution)/shard_map/all_gather | solution.py:17
  218.1 172.4 %all-to-all-start.1 = ((bf16[32,1280,80]{1,2,0:T(8,128)(2,1)}), bf16[32,1280,80]{1,2,0:T(8,128)(2,1)}, u32[]{:S(2)}, u32[]{:S(2)}) async-start(bf16[32,1280,80]{1,2,0:T(8,128)(2,1)} %broadcast_in_dim.2), calls=%async_computation.1 | async-start | bytes 13107200 | tf_op jit(solution)/shard_map/all_to_all | solution.py:31
  226.9 163.5 %copy-start.1 = (f32[320,1280]{1,0:T(8,128)S(1)}, f32[320,1280]{1,0:T(8,128)}, u32[]{:S(2)}) copy-start(f32[320,1280]{1,0:T(8,128)} %param.7) | copy-start | bytes 4915204
  226.9 163.5 %all-gather.5.cloned.1.call-start = ((), (), s32[]{:S(2)}) async-start(), calls=%async_computation.3 | async-start | bytes 2949120 | tf_op jit(solution)/shard_map/all_gather | solution.py:41
  232.6 29.5 %collective-permute-start = (bf16[40,32,80]{2,0,1:T(8,128)(2,1)S(1)}, bf16[40,32,80]{2,0,1:T(8,128)(2,1)S(1)}, u32[]{:S(2)}, u32[]{:S(2)}) collective-permute-start(bf16[40,32,80]{2,0,1:T(8,128)(2,1)S(1)} %pad_maximum_fusion.1), channel_id=1, source_target_pairs={{0,0},{1,32},{2,64},{3,96},{4,128},{5,160},{6,192},{7,224},{8,1},{... | collective-permute-start | bytes 614408 | tf_op jit(solution)/shard_map/ppermute | solution.py:40
  262.1 0.7 copy-start
Sparse Core Ops, SparseCore 0:
  9.2 87.8 all-gather.2
  263.0 127.4 all-gather.4

commit v5 on v1

--- a/solution.py
+++ b/solution.py
@@ -35,7 +35,9 @@
         for n in range(n_narrow):
             perm.append((w * n_narrow + n, (n * blocks + w // n_narrow) * n_narrow + w % n_narrow))
     left_piece = lax.ppermute(left_piece, ("wide", "narrow"), perm)
-    left_rows = lax.all_gather(left_piece, "narrow", axis=0, tiled=True)
+    left_rows = lax.all_to_all(
+        jnp.broadcast_to(left_piece[None], (n_narrow,) + left_piece.shape), "narrow", 0, 0, tiled=True
+    ).reshape((tile_rows,) + left_piece.shape[1:])
 
     update = lax.dot_general(
         left_rows, rc_all, (((1, 2), (0, 2)), ((), ())), preferred_element_type=jnp.float32

time: 364 us -> 390 us (1.071)
  blocking collectives: 0 us -> 65.7 us
  waiting for transfers between devices: 290 us -> 250 us
    all_to_all x0 -> x1, blocking collectives: none -> 65.7 us  [per_device(): lax.all_to_all(jnp.broadcast_to(left_piece[None], (n_narrow,) + left_piec...]
    all_gather x1 -> x0, waiting for transfers between devices: 40 us -> none  [per_device(): left_rows = lax.all_gather(left_piece, 'narrow', axis=0, tiled=True)]
  transfers between devices with their start and end apart: 5 -> 4, of which waited for: 5 -> 4; matrix products, arithmetic and copies ran while one was open for 7% -> 6% of each run, Pallas kernels for 0% -> 0%
where the time goes in v5:
time: 390 us; the launch traced here: 386 us
  waiting for transfers between devices  250 us (64%)
  blocking collectives  65.7 us (17%)
  matrix products  25.4 us (7%)
  starting transfers between devices  20 us (5%)
  between operations  13.5 us (3%)
  local copies, waits for them, and re-layouts  6.99 us (2%)
  other arithmetic  4.34 us (1%)
    all_gather x1, waiting for transfers between devices, per_device(): cmm_full = lax.all_gather(cmm_panel, 'narrow', axis=1, tiled=True)  109 us
    all_to_all x1, waiting for transfers between devices, per_device(): lax.all_to_all(z_part.reshape(n_wide, piece, z_part.shape[1]), 'wide', 0,...  89.3 us
    all_to_all x1, blocking collectives, per_device(): lax.all_to_all(jnp.broadcast_to(left_piece[None], (n_narrow,) + left_piec...  65.7 us
    ppermute x1, waiting for transfers between devices, per_device(): left_piece = lax.ppermute(left_piece, ('wide', 'narrow'), perm)  36.7 us
    dot_general x1, matrix products, per_device(): z_part = jnp.dot(r_matrix, cmm_full, preferred_element_type=jnp.float32)  17.8 us
    all_to_all x1, waiting for transfers between devices, per_device(): lax.all_to_all(jnp.broadcast_to(rc[None], (n_wide,) + rc.shape), 'wide',...  14.3 us
    all_to_all x1, starting transfers between devices, per_device(): lax.all_to_all(z_part.reshape(n_wide, piece, z_part.shape[1]), 'wide', 0,...  9.58 us
    all_to_all x1, starting transfers between devices, per_device(): lax.all_to_all(jnp.broadcast_to(rc[None], (n_wide,) + rc.shape), 'wide',...  8.46 us
  transfers between devices with their start and end apart: 4, of which 4 were waited for; matrix products, arithmetic and copies ran while one was open for 6% of the time, Pallas kernels for 0%

profile of v5, /device:TPU:42, one launch (start us, length us, event | category | flops | bytes accessed | tf_op | source)
XLA Modules:
  0.0 385.6 jit_solution(10979290387024833647)
XLA Ops:
  6.5 0.0 all-gather.2.cloned.1.call-start
  6.5 0.7 all-gather.2.cloned.1.call-update
  7.3 1.0 slice.9
  8.3 0.2 copy.13
  8.4 0.9 pad_maximum_fusion.1
  9.3 3.1 broadcast_in_dim.4
  12.4 8.5 %all-to-all-start.1 = ((bf16[32,1280,80]{1,2,0:T(8,128)(2,1)}), bf16[32,1280,80]{1,2,0:T(8,128)(2,1)}, u32[]{:S(2)}, u32[]{:S(2)}) async-start(bf16[32,1280,80]{1,2,0:T(8,128)(2,1)} %broadcast_in_dim.4), calls=%async_computation.1 | async-start | bytes 13107200 | tf_op jit(solution)/shard_map/all_to_all | solution.py:16
  20.9 108.7 %all-gather.2.cloned.1.call-done = bf16[3200,1280]{0,1:T(8,128)(2,1)} async-done(((bf16[3200,160]{0,1:T(8,128)(2,1)}), bf16[3200,1280]{0,1:T(8,128)(2,1)}) %all-gather.2.cloned.1.call-update) | async-done | bytes 8192016 | tf_op jit(solution)/shard_map/all_gather | solution.py:20
  129.5 17.8 %fusion.2 = f32[1280,1280]{1,0:T(8,128)} fusion(bf16[1280,3200]{1,0:T(8,128)(2,1)} %param.4, bf16[3200,1280]{0,1:T(8,128)(2,1)} %all-gather.2.cloned.1.call-done), kind=kOutput, calls=%fused_computation.8 | convolution fusion | flops 10485760000 | bytes 22937600 | tf_op jit(solution)/shard_map/dot_general | solution.py:21
  147.3 14.3 %all-to-all-done.1 = bf16[32,1280,80]{1,2,0:T(8,128)(2,1)} async-done(((bf16[32,1280,80]{1,2,0:T(8,128)(2,1)}), bf16[32,1280,80]{1,2,0:T(8,128)(2,1)}, u32[]{:S(2)}, u32[]{:S(2)}) %all-to-all-start.1) | async-done | bytes 6553632 | tf_op jit(solution)/shard_map/all_to_all | solution.py:16
  161.6 9.6 %all-to-all-start = ((f32[32,40,1280]{2,1,0:T(8,128)}), f32[32,40,1280]{2,1,0:T(8,128)}, u32[]{:S(2)}, u32[]{:S(2)}) async-start(f32[32,40,1280]{2,1,0:T(8,128)} %bitcast.12), calls=%async_computation | async-start | bytes 13107200 | tf_op jit(solution)/shard_map/all_to_all | solution.py:23
  171.2 1.6 dynamic-slice_bitcast_fusion
  172.8 89.3 %all-to-all-done = f32[32,40,1280]{2,1,0:T(8,128)} async-done(((f32[32,40,1280]{2,1,0:T(8,128)}), f32[32,40,1280]{2,1,0:T(8,128)}, u32[]{:S(2)}, u32[]{:S(2)}) %all-to-all-start) | async-done | bytes 6553632 | tf_op jit(solution)/shard_map/all_to_all | solution.py:23
  262.1 3.2 reduce_sum.9
  265.3 0.0 copy-start
  265.3 0.2 copy.9
  265.5 0.1 subtract_convert_fusion
  265.6 0.1 pad_maximum_fusion
  265.8 0.5 copy.11
  266.3 1.9 collective-permute-start
  268.2 36.7 %collective-permute-done = bf16[40,32,80]{2,1,0:T(8,128)(2,1)S(1)} collective-permute-done((bf16[40,32,80]{2,1,0:T(8,128)(2,1)S(1)}, bf16[40,32,80]{2,1,0:T(8,128)(2,1)S(1)}, u32[]{:S(2)}, u32[]{:S(2)}) %collective-permute-start) | collective-permute-done | bytes 204832 | tf_op jit(solution)/shard_map/ppermute | solution.py:37
  304.9 0.4 broadcast_in_dim.5
  305.4 65.7 %all_to_all.15 = bf16[8,40,32,80]{3,2,1,0:T(8,128)(2,1)S(1)} all-to-all(bf16[8,40,32,80]{3,2,1,0:T(8,128)(2,1)S(1)} %broadcast_in_dim.5), channel_id=1, replica_groups=mesh['wide'=32,'narrow'=8] {'narrow'}, dimensions={0} | all-to-all | bytes 3276800 | tf_op jit(solution)/shard_map/all_to_all | solution.py:38
  371.1 0.0 copy-done
  371.1 7.6 %fusion = f32[320,1280]{1,0:T(8,128)} fusion(f32[320,1280]{1,0:T(8,128)S(1)} %copy-done, bf16[32,1280,80]{1,2,0:T(8,128)(2,1)} %all-to-all-done.1, bf16[320,32,80]{2,1,0:T(8,128)(2,1)S(1)} %bitcast.13), kind=kOutput, calls=%fused_computation.1 | convolution fusion | flops 2097561600 | bytes 11468800 | tf_op jit(solution)/shard_map/dot_general | solution.py:42
  (1 shorter events, 0.0 us)
Async XLA Ops:
  6.5 123.0 %all-gather.2.cloned.1.call-start = ((), (), s32[]{:S(2)}) async-start(), calls=%async_computation.3 | async-start | bytes 9216000 | tf_op jit(solution)/shard_map/all_gather | solution.py:20
  12.4 149.2 %all-to-all-start.1 = ((bf16[32,1280,80]{1,2,0:T(8,128)(2,1)}), bf16[32,1280,80]{1,2,0:T(8,128)(2,1)}, u32[]{:S(2)}, u32[]{:S(2)}) async-start(bf16[32,1280,80]{1,2,0:T(8,128)(2,1)} %broadcast_in_dim.4), calls=%async_computation.1 | async-start | bytes 13107200 | tf_op jit(solution)/shard_map/all_to_all | solution.py:16
  161.6 100.5 %all-to-all-start = ((f32[32,40,1280]{2,1,0:T(8,128)}), f32[32,40,1280]{2,1,0:T(8,128)}, u32[]{:S(2)}, u32[]{:S(2)}) async-start(f32[32,40,1280]{2,1,0:T(8,128)} %bitcast.12), calls=%async_computation | async-start | bytes 13107200 | tf_op jit(solution)/shard_map/all_to_all | solution.py:23
  265.3 105.8 %copy-start = (f32[320,1280]{1,0:T(8,128)S(1)}, f32[320,1280]{1,0:T(8,128)}, u32[]{:S(2)}) copy-start(f32[320,1280]{1,0:T(8,128)} %param.7) | copy-start | bytes 4915204
  266.3 38.7 %collective-permute-start = (bf16[40,32,80]{2,1,0:T(8,128)(2,1)S(1)}, bf16[40,32,80]{2,1,0:T(8,128)(2,1)S(1)}, u32[]{:S(2)}, u32[]{:S(2)}) collective-permute-start(bf16[40,32,80]{2,1,0:T(8,128)(2,1)S(1)} %copy.11), channel_id=1, source_target_pairs={{0,0},{1,32},{2,64},{3,96},{4,128},{5,160},{6,192},{7,224},{8,1},{... | collective-permute-start | bytes 614408 | tf_op jit(solution)/shard_map/ppermute | solution.py:37
Sparse Core Ops, SparseCore 0:
  9.2 120.3 all-gather.1

commit v6 on v1

--- a/solution.py
+++ b/solution.py
@@ -2,6 +2,40 @@
 import jax.numpy as jnp
 from jax import lax
 from jax.sharding import PartitionSpec as P
+
+
+def _position(w, n, n_wide, n_narrow):
+    if (n_wide, n_narrow) == (32, 8):
+        x, rest = divmod(w, 8)
+        y, z_lo = divmod(rest, 2)
+        z_hi, core = divmod(n, 2)
+        return (x, y, 2 * z_hi + z_lo), (4, 4, 8)
+    return (w, n), (n_wide, n_narrow)
+
+
+def _hops(a, b, n_wide, n_narrow):
+    (pa, sizes), (pb, _) = _position(*a, n_wide, n_narrow), _position(*b, n_wide, n_narrow)
+    return sum(min(abs(u - v), size - abs(u - v)) for u, v, size in zip(pa, pb, sizes))
+
+
+def _routes(n_wide, n_narrow):
+    blocks = n_wide // n_narrow
+    pieces, perm = [], []
+    for n0 in range(n_narrow):
+        pairs = sorted(
+            (_hops((w, n0), (n0 * blocks + k, m), n_wide, n_narrow), w, k, m)
+            for w in range(n_wide) for k in range(blocks) for m in range(n_narrow)
+        )
+        taken_w, taken_t, row = set(), set(), [0] * n_wide
+        for _, w, k, m in pairs:
+            if w in taken_w or (k, m) in taken_t:
+                continue
+            taken_w.add(w)
+            taken_t.add((k, m))
+            row[w] = k * n_narrow + m
+            perm.append((w * n_narrow + n0, (n0 * blocks + k) * n_narrow + m))
+        pieces.append(row)
+    return pieces, perm
 
 
 def per_device(r_matrix, cmm_panel, ctm_panel, cee_in, n_wide, n_narrow):
@@ -17,23 +51,25 @@
         jnp.broadcast_to(rc[None], (n_wide,) + rc.shape), "wide", 0, 0, tiled=True
     )
 
+    pieces, perm = _routes(n_wide, n_narrow)
+    pieces = jnp.asarray(pieces, jnp.int32)
+    mine = pieces[narrow_index, wide_index]
+    r_sent = jnp.take(
+        r_matrix.reshape(n_wide, piece, r_matrix.shape[1]), pieces[narrow_index], axis=0
+    ).reshape(r_matrix.shape)
+
     cmm_full = lax.all_gather(cmm_panel, "narrow", axis=1, tiled=True)
-    z_part = jnp.dot(r_matrix, cmm_full, preferred_element_type=jnp.float32)
+    z_part = jnp.dot(r_sent, cmm_full, preferred_element_type=jnp.float32)
 
     z_recv = lax.all_to_all(
         z_part.reshape(n_wide, piece, z_part.shape[1]), "wide", 0, 0, tiled=True
     )
     z_mine = jnp.sum(z_recv, axis=0).reshape(piece, n_wide, panel_width)
-    rc_rows = lax.dynamic_slice_in_dim(rc_all, wide_index * piece, piece, 1)
+    rc_rows = lax.dynamic_slice_in_dim(rc_all, mine * piece, piece, 1)
     rc_rows = jnp.transpose(rc_rows, (1, 0, 2))
     a_piece = (z_mine - rc_rows[:, :, panel_width:].astype(jnp.float32)).astype(jnp.bfloat16)
     left_piece = jnp.concatenate([a_piece, -rc_rows[:, :, :panel_width]], axis=2)
 
-    blocks = n_wide // n_narrow
-    perm = []
-    for w in range(n_wide):
-        for n in range(n_narrow):
-            perm.append((w * n_narrow + n, (n * blocks + w // n_narrow) * n_narrow + w % n_narrow))
     left_piece = lax.ppermute(left_piece, ("wide", "narrow"), perm)
     left_rows = lax.all_gather(left_piece, "narrow", axis=0, tiled=True)
 

time: 364 us -> 357 us (0.981)
  waiting for transfers between devices: 290 us -> 254 us
  starting transfers between devices: 20 us -> 35.5 us
  local copies, waits for them, and re-layouts: 7.4 us -> 17.7 us
    ppermute x1, waiting for transfers between devices: 36.7 us -> 7.76 us  [per_device(): left_piece = lax.ppermute(left_piece, ('wide', 'narrow'), perm)]
    ppermute x1, starting transfers between devices: 1.92 us -> 17.4 us  [per_device(): left_piece = lax.ppermute(left_piece, ('wide', 'narrow'), perm)]
    all_gather x1, waiting for transfers between devices: 109 us -> 98.2 us  [per_device(): cmm_full = lax.all_gather(cmm_panel, 'narrow', axis=1, tiled=True)]
    gather x0 -> x1, local copies, waits for them, and re-layouts: none -> 8.99 us  [per_device(): jnp.take(r_matrix.reshape(n_wide, piece, r_matrix.shape[1]), pieces[narro...]
    all_gather x1, waiting for transfers between devices: 40 us -> 46.1 us  [per_device(): left_rows = lax.all_gather(left_piece, 'narrow', axis=0, tiled=True)]
  transfers between devices with their start and end apart: 5 -> 5, of which waited for: 5 -> 5; matrix products, arithmetic and copies ran while one was open for 7% -> 10% of each run, Pallas kernels for 0% -> 0%
where the time goes in v6:
time: 357 us; the launch traced here: 354 us
  waiting for transfers between devices  254 us (71%)
  starting transfers between devices  35.5 us (10%)
  matrix products  26.2 us (7%)
  local copies, waits for them, and re-layouts  17.7 us (5%)
  between operations  14.2 us (4%)
  other arithmetic  5.75 us (2%)
    all_gather x1, waiting for transfers between devices, per_device(): cmm_full = lax.all_gather(cmm_panel, 'narrow', axis=1, tiled=True)  98.2 us
    all_to_all x1, waiting for transfers between devices, per_device(): lax.all_to_all(z_part.reshape(n_wide, piece, z_part.shape[1]), 'wide', 0,...  87.2 us
    all_gather x1, waiting for transfers between devices, per_device(): left_rows = lax.all_gather(left_piece, 'narrow', axis=0, tiled=True)  46.1 us
    dot_general x1, matrix products, per_device(): z_part = jnp.dot(r_sent, cmm_full, preferred_element_type=jnp.float32)  17.8 us
    ppermute x1, starting transfers between devices, per_device(): left_piece = lax.ppermute(left_piece, ('wide', 'narrow'), perm)  17.4 us
    all_to_all x1, waiting for transfers between devices, per_device(): lax.all_to_all(jnp.broadcast_to(rc[None], (n_wide,) + rc.shape), 'wide',...  14.3 us
    all_to_all x1, starting transfers between devices, per_device(): lax.all_to_all(z_part.reshape(n_wide, piece, z_part.shape[1]), 'wide', 0,...  9.53 us
    gather x1, local copies, waits for them, and re-layouts, per_device(): jnp.take(r_matrix.reshape(n_wide, piece, r_matrix.shape[1]), pieces[narro...  8.99 us
  transfers between devices with their start and end apart: 5, of which 5 were waited for; matrix products, arithmetic and copies ran while one was open for 10% of the time, Pallas kernels for 0%

profile of v6, /device:TPU:42, one launch (start us, length us, event | category | flops | bytes accessed | tf_op | source)
XLA Modules:
  0.0 353.6 jit_solution(2708746364616048224)
XLA Ops:
  6.5 0.0 all-gather.3.cloned.1.call-start
  6.5 0.7 all-gather.3.cloned.1.call-update
  7.3 1.0 slice.9
  8.3 0.2 copy.12
  8.4 0.9 pad_maximum_fusion.1
  9.3 3.1 broadcast_in_dim.18
  12.5 8.5 %all-to-all-start.1 = ((bf16[32,1280,80]{1,2,0:T(8,128)(2,1)}), bf16[32,1280,80]{1,2,0:T(8,128)(2,1)}, u32[]{:S(2)}, u32[]{:S(2)}) async-start(bf16[32,1280,80]{1,2,0:T(8,128)(2,1)} %broadcast_in_dim.18), calls=%async_computation.1 | async-start | bytes 13107200 | tf_op jit(solution)/shard_map/all_to_all | solution.py:50
  20.9 0.7 fusion.7
  21.6 9.0 %gather_fusion = bf16[32,40,3200]{2,1,0:T(8,128)(2,1)} fusion(bf16[32,40,3200]{2,1,0:T(8,128)(2,1)} %bitcast.19, s32[1024]{0:T(1024)S(1)} %pad_clamp_fusion), kind=kCustom, calls=%fused_computation | custom fusion | bytes 16384128 | tf_op jit(solution)/shard_map/jit(_take)/gather | solution.py:57
  30.6 0.7 compare_and_fusion
  31.3 98.2 %all-gather.3.cloned.1.call-done = bf16[3200,1280]{0,1:T(8,128)(2,1)} async-done(((bf16[3200,160]{0,1:T(8,128)(2,1)}), bf16[3200,1280]{0,1:T(8,128)(2,1)}) %all-gather.3.cloned.1.call-update) | async-done | bytes 8192016 | tf_op jit(solution)/shard_map/all_gather | solution.py:61
  129.5 17.8 %fusion = f32[32,40,1280]{2,1,0:T(8,128)} fusion(bf16[3200,1280]{0,1:T(8,128)(2,1)} %all-gather.3.cloned.1.call-done, bf16[32,40,3200]{2,1,0:T(8,128)(2,1)} %gather_fusion, pred[32]{0:T(512)(128)(4,1)S(1)} %compare_and_fusion), kind=kOutput, calls=%fused_computation.1 | convolution fusion | flops 10489856000 | bytes 22937632 | tf_op jit(solution)/shard_map/dot_general | solution.py:62
  147.3 14.3 %all-to-all-done.1 = bf16[32,1280,80]{1,2,0:T(8,128)(2,1)} async-done(((bf16[32,1280,80]{1,2,0:T(8,128)(2,1)}), bf16[32,1280,80]{1,2,0:T(8,128)(2,1)}, u32[]{:S(2)}, u32[]{:S(2)}) %all-to-all-start.1) | async-done | bytes 6553632 | tf_op jit(solution)/shard_map/all_to_all | solution.py:50
  161.6 9.5 %all-to-all-start = ((f32[32,40,1280]{2,1,0:T(8,128)}), f32[32,40,1280]{2,1,0:T(8,128)}, u32[]{:S(2)}, u32[]{:S(2)}) async-start(f32[32,40,1280]{2,1,0:T(8,128)} %fusion), calls=%async_computation | async-start | bytes 13107200 | tf_op jit(solution)/shard_map/all_to_all | solution.py:64
  171.2 0.0 all-gather.5.cloned.1.call-start
  171.2 1.3 dynamic_slice.10
  173.2 0.0 copy-start.1
  173.2 1.7 dynamic-slice_bitcast_fusion
  174.9 87.2 %all-to-all-done = f32[32,40,1280]{2,1,0:T(8,128)} async-done(((f32[32,40,1280]{2,1,0:T(8,128)}), f32[32,40,1280]{2,1,0:T(8,128)}, u32[]{:S(2)}, u32[]{:S(2)}) %all-to-all-start) | async-done | bytes 6553632 | tf_op jit(solution)/shard_map/all_to_all | solution.py:64
  262.1 3.2 reduce_sum.9
  265.3 0.2 copy.8
  265.5 0.1 subtract_convert_fusion
  265.6 0.1 pad_maximum_fusion
  265.7 0.5 copy.10
  266.3 17.4 %collective-permute-start = (bf16[40,32,80]{2,1,0:T(8,128)(2,1)S(1)}, bf16[40,32,80]{2,1,0:T(8,128)(2,1)S(1)}, u32[]{:S(2)}, u32[]{:S(2)}) collective-permute-start(bf16[40,32,80]{2,1,0:T(8,128)(2,1)S(1)} %copy.10), channel_id=1, source_target_pairs={{0,0},{8,8},{16,16},{24,24},{32,17},{40,25},{48,1},{56,9},{64,14},... | collective-permute-start | bytes 614408 | tf_op jit(solution)/shard_map/ppermute | solution.py:73
  283.7 7.8 %collective-permute-done = bf16[40,32,80]{2,1,0:T(8,128)(2,1)S(1)} collective-permute-done((bf16[40,32,80]{2,1,0:T(8,128)(2,1)S(1)}, bf16[40,32,80]{2,1,0:T(8,128)(2,1)S(1)}, u32[]{:S(2)}, u32[]{:S(2)}) %collective-permute-start) | collective-permute-done | bytes 204832 | tf_op jit(solution)/shard_map/ppermute | solution.py:73
  291.5 0.0 copy-start
  291.5 0.7 copy-done
  292.2 0.0 all-gather.5.cloned.1.call-update
  292.2 46.1 %all-gather.5.cloned.1.call-done = bf16[320,32,80]{2,1,0:T(8,128)(2,1)} async-done(((bf16[40,32,80]{2,1,0:T(8,128)(2,1)}), bf16[320,32,80]{2,1,0:T(8,128)(2,1)}) %all-gather.5.cloned.1.call-update) | async-done | bytes 1638416 | tf_op jit(solution)/shard_map/all_gather | solution.py:74
  338.3 0.0 copy-done.1
  338.3 8.4 %fusion.5 = f32[320,1280]{1,0:T(8,128)} fusion(f32[320,1280]{1,0:T(8,128)S(1)} %copy-done.1, bf16[32,1280,80]{1,2,0:T(8,128)(2,1)} %all-to-all-done.1, bf16[320,32,80]{2,1,0:T(8,128)(2,1)} %all-gather.5.cloned.1.call-done), kind=kOutput, calls=%fused_computation.7 | convolution fusion | flops 2097561600 | bytes 11468800 | tf_op jit(solution)/shard_map/dot_general | solution.py:76
  (2 shorter events, 0.1 us)
Async XLA Ops:
  6.5 123.0 %all-gather.3.cloned.1.call-start = ((), (), s32[]{:S(2)}) async-start(), calls=%async_computation.2 | async-start | bytes 9216000 | tf_op jit(solution)/shard_map/all_gather | solution.py:61
  12.5 149.2 %all-to-all-start.1 = ((bf16[32,1280,80]{1,2,0:T(8,128)(2,1)}), bf16[32,1280,80]{1,2,0:T(8,128)(2,1)}, u32[]{:S(2)}, u32[]{:S(2)}) async-start(bf16[32,1280,80]{1,2,0:T(8,128)(2,1)} %broadcast_in_dim.18), calls=%async_computation.1 | async-start | bytes 13107200 | tf_op jit(solution)/shard_map/all_to_all | solution.py:50
  161.6 100.5 %all-to-all-start = ((f32[32,40,1280]{2,1,0:T(8,128)}), f32[32,40,1280]{2,1,0:T(8,128)}, u32[]{:S(2)}, u32[]{:S(2)}) async-start(f32[32,40,1280]{2,1,0:T(8,128)} %fusion), calls=%async_computation | async-start | bytes 13107200 | tf_op jit(solution)/shard_map/all_to_all | solution.py:64
  171.2 167.1 %all-gather.5.cloned.1.call-start = ((), (), s32[]{:S(2)}) async-start(), calls=%async_computation.3 | async-start | bytes 2949120 | tf_op jit(solution)/shard_map/all_gather | solution.py:74
  173.2 165.2 %copy-start.1 = (f32[320,1280]{1,0:T(8,128)S(1)}, f32[320,1280]{1,0:T(8,128)}, u32[]{:S(2)}) copy-start(f32[320,1280]{1,0:T(8,128)} %param.8) | copy-start | bytes 4915204
  266.3 25.2 %collective-permute-start = (bf16[40,32,80]{2,1,0:T(8,128)(2,1)S(1)}, bf16[40,32,80]{2,1,0:T(8,128)(2,1)S(1)}, u32[]{:S(2)}, u32[]{:S(2)}) collective-permute-start(bf16[40,32,80]{2,1,0:T(8,128)(2,1)S(1)} %copy.10), channel_id=1, source_target_pairs={{0,0},{8,8},{16,16},{24,24},{32,17},{40,25},{48,1},{56,9},{64,14},... | collective-permute-start | bytes 614408 | tf_op jit(solution)/shard_map/ppermute | solution.py:73
  291.5 0.7 copy-start
Sparse Core Ops, SparseCore 0:
  9.2 120.3 all-gather.2
  292.3 45.9 all-gather.4

commit v7 on v6

--- a/solution.py
+++ b/solution.py
@@ -73,8 +73,12 @@
     left_piece = lax.ppermute(left_piece, ("wide", "narrow"), perm)
     left_rows = lax.all_gather(left_piece, "narrow", axis=0, tiled=True)
 
+    right = lax.optimization_barrier(
+        jnp.transpose(rc_all, (1, 0, 2)).reshape(slope_rows, n_wide * 2 * panel_width)
+    )
     update = lax.dot_general(
-        left_rows, rc_all, (((1, 2), (0, 2)), ((), ())), preferred_element_type=jnp.float32
+        left_rows.reshape(tile_rows, -1), right, (((1,), (1,)), ((), ())),
+        preferred_element_type=jnp.float32,
     )
     return cee_in + update
 

time: 357 us -> 359 us (level)
  no operation moved by 1% of the time
where the time goes in v7:
time: 359 us; the launch traced here: 355 us
  waiting for transfers between devices  255 us (71%)
  starting transfers between devices  35.3 us (10%)
  matrix products  24.6 us (7%)
  local copies, waits for them, and re-layouts  21 us (6%)
  between operations  14.2 us (4%)
  other arithmetic  5.75 us (2%)
    all_gather x1, waiting for transfers between devices, per_device(): cmm_full = lax.all_gather(cmm_panel, 'narrow', axis=1, tiled=True)  98.2 us
    all_to_all x1, waiting for transfers between devices, per_device(): lax.all_to_all(z_part.reshape(n_wide, piece, z_part.shape[1]), 'wide', 0,...  87.3 us
    all_gather x1, waiting for transfers between devices, per_device(): left_rows = lax.all_gather(left_piece, 'narrow', axis=0, tiled=True)  47.7 us
    dot_general x1, matrix products, per_device(): z_part = jnp.dot(r_sent, cmm_full, preferred_element_type=jnp.float32)  17.8 us
    ppermute x1, starting transfers between devices, per_device(): left_piece = lax.ppermute(left_piece, ('wide', 'narrow'), perm)  17.3 us
    all_to_all x1, waiting for transfers between devices, per_device(): lax.all_to_all(jnp.broadcast_to(rc[None], (n_wide,) + rc.shape), 'wide',...  14.3 us
    all_to_all x1, starting transfers between devices, per_device(): lax.all_to_all(z_part.reshape(n_wide, piece, z_part.shape[1]), 'wide', 0,...  9.51 us
    gather x1, local copies, waits for them, and re-layouts, per_device(): jnp.take(r_matrix.reshape(n_wide, piece, r_matrix.shape[1]), pieces[narro...  8.97 us
  transfers between devices with their start and end apart: 5, of which 5 were waited for; matrix products, arithmetic and copies ran while one was open for 10% of the time, Pallas kernels for 0%

profile of v7, /device:TPU:42, one launch (start us, length us, event | category | flops | bytes accessed | tf_op | source)
XLA Modules:
  0.0 355.4 jit_solution(11727490373967747587)
XLA Ops:
  6.5 0.0 all-gather.3.cloned.1.call-start
  6.5 0.7 all-gather.3.cloned.1.call-update
  7.3 1.0 slice.9
  8.3 0.2 copy.14
  8.4 0.9 pad_maximum_fusion.1
  9.3 3.1 broadcast_in_dim.18
  12.5 8.5 %all-to-all-start.1 = ((bf16[32,1280,80]{1,2,0:T(8,128)(2,1)}), bf16[32,1280,80]{1,2,0:T(8,128)(2,1)}, u32[]{:S(2)}, u32[]{:S(2)}) async-start(bf16[32,1280,80]{1,2,0:T(8,128)(2,1)} %broadcast_in_dim.18), calls=%async_computation.1 | async-start | bytes 13107200 | tf_op jit(solution)/shard_map/all_to_all | solution.py:50
  20.9 0.7 fusion.5
  21.6 9.0 %gather_fusion = bf16[32,40,3200]{2,1,0:T(8,128)(2,1)} fusion(bf16[32,40,3200]{2,1,0:T(8,128)(2,1)} %bitcast.21, s32[1024]{0:T(1024)S(1)} %pad_clamp_fusion), kind=kCustom, calls=%fused_computation | custom fusion | bytes 16384128 | tf_op jit(solution)/shard_map/jit(_take)/gather | solution.py:57
  30.6 0.7 compare_and_fusion
  31.3 98.2 %all-gather.3.cloned.1.call-done = bf16[3200,1280]{0,1:T(8,128)(2,1)} async-done(((bf16[3200,160]{0,1:T(8,128)(2,1)}), bf16[3200,1280]{0,1:T(8,128)(2,1)}) %all-gather.3.cloned.1.call-update) | async-done | bytes 8192016 | tf_op jit(solution)/shard_map/all_gather | solution.py:61
  129.5 17.8 %fusion = f32[32,40,1280]{2,1,0:T(8,128)} fusion(bf16[3200,1280]{0,1:T(8,128)(2,1)} %all-gather.3.cloned.1.call-done, bf16[32,40,3200]{2,1,0:T(8,128)(2,1)} %gather_fusion, pred[32]{0:T(512)(128)(4,1)S(1)} %compare_and_fusion), kind=kOutput, calls=%fused_computation.1 | convolution fusion | flops 10489856000 | bytes 22937632 | tf_op jit(solution)/shard_map/dot_general | solution.py:62
  147.3 14.3 %all-to-all-done.1 = bf16[32,1280,80]{1,2,0:T(8,128)(2,1)} async-done(((bf16[32,1280,80]{1,2,0:T(8,128)(2,1)}), bf16[32,1280,80]{1,2,0:T(8,128)(2,1)}, u32[]{:S(2)}, u32[]{:S(2)}) %all-to-all-start.1) | async-done | bytes 6553632 | tf_op jit(solution)/shard_map/all_to_all | solution.py:50
  161.7 9.5 %all-to-all-start = ((f32[32,40,1280]{2,1,0:T(8,128)}), f32[32,40,1280]{2,1,0:T(8,128)}, u32[]{:S(2)}, u32[]{:S(2)}) async-start(f32[32,40,1280]{2,1,0:T(8,128)} %fusion), calls=%async_computation | async-start | bytes 13107200 | tf_op jit(solution)/shard_map/all_to_all | solution.py:64
  171.2 0.0 all-gather.5.cloned.1.call-start
  171.2 1.3 dynamic_slice.10
  173.2 1.6 dynamic-slice_bitcast_fusion
  174.8 87.3 %all-to-all-done = f32[32,40,1280]{2,1,0:T(8,128)} async-done(((f32[32,40,1280]{2,1,0:T(8,128)}), f32[32,40,1280]{2,1,0:T(8,128)}, u32[]{:S(2)}, u32[]{:S(2)}) %all-to-all-start) | async-done | bytes 6553632 | tf_op jit(solution)/shard_map/all_to_all | solution.py:64
  262.1 3.2 reduce_sum.9
  265.3 0.2 copy.13
  265.5 0.1 subtract_convert_fusion
  265.6 0.1 pad_maximum_fusion
  265.8 0.5 copy.11
  266.3 17.3 %collective-permute-start = (bf16[40,32,80]{2,1,0:T(8,128)(2,1)S(1)}, bf16[40,32,80]{2,1,0:T(8,128)(2,1)S(1)}, u32[]{:S(2)}, u32[]{:S(2)}) collective-permute-start(bf16[40,32,80]{2,1,0:T(8,128)(2,1)S(1)} %copy.11), channel_id=1, source_target_pairs={{0,0},{8,8},{16,16},{24,24},{32,17},{40,25},{48,1},{56,9},{64,14},... | collective-permute-start | bytes 614408 | tf_op jit(solution)/shard_map/ppermute | solution.py:73
  283.5 6.4 %collective-permute-done = bf16[40,32,80]{2,1,0:T(8,128)(2,1)S(1)} collective-permute-done((bf16[40,32,80]{2,1,0:T(8,128)(2,1)S(1)}, bf16[40,32,80]{2,1,0:T(8,128)(2,1)S(1)}, u32[]{:S(2)}, u32[]{:S(2)}) %collective-permute-start) | collective-permute-done | bytes 204832 | tf_op jit(solution)/shard_map/ppermute | solution.py:73
  289.9 0.0 copy-start
  290.0 0.7 copy-done
  290.7 0.0 all-gather.5.cloned.1.call-update
  290.7 47.7 %all-gather.5.cloned.1.call-done = bf16[320,32,80]{2,1,0:T(8,128)(2,1)} async-done(((bf16[40,32,80]{2,1,0:T(8,128)(2,1)}), bf16[320,32,80]{2,1,0:T(8,128)(2,1)}) %all-gather.5.cloned.1.call-update) | async-done | bytes 1638416 | tf_op jit(solution)/shard_map/all_gather | solution.py:74
  338.3 3.4 copy.12
  341.8 6.8 %convolution_add_fusion = f32[320,1280]{1,0:T(8,128)} fusion(f32[320,1280]{1,0:T(8,128)} %param.8, bf16[320,2560]{0,1:T(8,128)(2,1)S(1)} %bitcast.20, bf16[1280,2560]{0,1:T(8,128)(2,1)} %bitcast.10), kind=kOutput, calls=%fused_computation.6 | convolution fusion | flops 2097561600 | bytes 11468800 | tf_op jit(solution)/shard_map/dot_general | solution.py:79
  (2 shorter events, 0.1 us)
Async XLA Ops:
  6.5 123.0 %all-gather.3.cloned.1.call-start = ((), (), s32[]{:S(2)}) async-start(), calls=%async_computation.2 | async-start | bytes 9216000 | tf_op jit(solution)/shard_map/all_gather | solution.py:61
  12.5 149.2 %all-to-all-start.1 = ((bf16[32,1280,80]{1,2,0:T(8,128)(2,1)}), bf16[32,1280,80]{1,2,0:T(8,128)(2,1)}, u32[]{:S(2)}, u32[]{:S(2)}) async-start(bf16[32,1280,80]{1,2,0:T(8,128)(2,1)} %broadcast_in_dim.18), calls=%async_computation.1 | async-start | bytes 13107200 | tf_op jit(solution)/shard_map/all_to_all | solution.py:50
  161.7 100.4 %all-to-all-start = ((f32[32,40,1280]{2,1,0:T(8,128)}), f32[32,40,1280]{2,1,0:T(8,128)}, u32[]{:S(2)}, u32[]{:S(2)}) async-start(f32[32,40,1280]{2,1,0:T(8,128)} %fusion), calls=%async_computation | async-start | bytes 13107200 | tf_op jit(solution)/shard_map/all_to_all | solution.py:64
  171.2 167.2 %all-gather.5.cloned.1.call-start = ((), (), s32[]{:S(2)}) async-start(), calls=%async_computation.3 | async-start | bytes 2949120 | tf_op jit(solution)/shard_map/all_gather | solution.py:74
  266.3 23.7 %collective-permute-start = (bf16[40,32,80]{2,1,0:T(8,128)(2,1)S(1)}, bf16[40,32,80]{2,1,0:T(8,128)(2,1)S(1)}, u32[]{:S(2)}, u32[]{:S(2)}) collective-permute-start(bf16[40,32,80]{2,1,0:T(8,128)(2,1)S(1)} %copy.11), channel_id=1, source_target_pairs={{0,0},{8,8},{16,16},{24,24},{32,17},{40,25},{48,1},{56,9},{64,14},... | collective-permute-start | bytes 614408 | tf_op jit(solution)/shard_map/ppermute | solution.py:73
  289.9 0.7 copy-start
Sparse Core Ops, SparseCore 0:
  9.2 120.3 all-gather.2
  290.8 47.4 all-gather.4

commit v8 on v6

--- a/solution.py
+++ b/solution.py
@@ -70,8 +70,9 @@
     a_piece = (z_mine - rc_rows[:, :, panel_width:].astype(jnp.float32)).astype(jnp.bfloat16)
     left_piece = jnp.concatenate([a_piece, -rc_rows[:, :, :panel_width]], axis=2)
 
-    left_piece = lax.ppermute(left_piece, ("wide", "narrow"), perm)
-    left_rows = lax.all_gather(left_piece, "narrow", axis=0, tiled=True)
+    shape = left_piece.shape
+    left_piece = lax.ppermute(left_piece.reshape(piece, -1), ("wide", "narrow"), perm)
+    left_rows = lax.all_gather(left_piece, "narrow", axis=0, tiled=True).reshape((tile_rows,) + shape[1:])
 
     update = lax.dot_general(
         left_rows, rc_all, (((1, 2), (0, 2)), ((), ())), preferred_element_type=jnp.float32

time: 357 us -> 348 us (0.975)
  waiting for transfers between devices: 254 us -> 245 us
    all_gather x1, waiting for transfers between devices: 46.1 us -> 40.9 us  [per_device(): lax.all_gather(left_piece, 'narrow', axis=0, tiled=True)]
    ppermute x1, waiting for transfers between devices: 7.76 us -> 3.25 us  [per_device(): lax.ppermute(left_piece.reshape(piece, -1), ('wide', 'narrow'), perm)]
    all_gather x0 -> x1, local copies, waits for them, and re-layouts: none -> 3.6 us  [per_device(): lax.all_gather(left_piece, 'narrow', axis=0, tiled=True)]
  transfers between devices with their start and end apart: 5 -> 5, of which waited for: 5 -> 5; matrix products, arithmetic and copies ran while one was open for 10% -> 11% of each run, Pallas kernels for 0% -> 0%
where the time goes in v8:
time: 348 us; the launch traced here: 345 us
  waiting for transfers between devices  245 us (70%)
  starting transfers between devices  35.3 us (10%)
  matrix products  24.6 us (7%)
  local copies, waits for them, and re-layouts  20.9 us (6%)
  between operations  14.2 us (4%)
  other arithmetic  5.75 us (2%)
    all_gather x1, waiting for transfers between devices, per_device(): cmm_full = lax.all_gather(cmm_panel, 'narrow', axis=1, tiled=True)  98.2 us
    all_to_all x1, waiting for transfers between devices, per_device(): lax.all_to_all(z_part.reshape(n_wide, piece, z_part.shape[1]), 'wide', 0,...  87.3 us
    all_gather x1, waiting for transfers between devices, per_device(): lax.all_gather(left_piece, 'narrow', axis=0, tiled=True)  40.9 us
    dot_general x1, matrix products, per_device(): z_part = jnp.dot(r_sent, cmm_full, preferred_element_type=jnp.float32)  17.8 us
    ppermute x1, starting transfers between devices, per_device(): lax.ppermute(left_piece.reshape(piece, -1), ('wide', 'narrow'), perm)  17.3 us
    all_to_all x1, waiting for transfers between devices, per_device(): lax.all_to_all(jnp.broadcast_to(rc[None], (n_wide,) + rc.shape), 'wide',...  14.3 us
    all_to_all x1, starting transfers between devices, per_device(): lax.all_to_all(z_part.reshape(n_wide, piece, z_part.shape[1]), 'wide', 0,...  9.51 us
    gather x1, local copies, waits for them, and re-layouts, per_device(): jnp.take(r_matrix.reshape(n_wide, piece, r_matrix.shape[1]), pieces[narro...  8.97 us
  transfers between devices with their start and end apart: 5, of which 5 were waited for; matrix products, arithmetic and copies ran while one was open for 11% of the time, Pallas kernels for 0%

profile of v8, /device:TPU:42, one launch (start us, length us, event | category | flops | bytes accessed | tf_op | source)
XLA Modules:
  0.0 345.4 jit_solution(5478650772908267630)
XLA Ops:
  6.5 0.0 all-gather.3.cloned.1.call-start
  6.5 0.7 all-gather.3.cloned.1.call-update
  7.3 1.0 slice.9
  8.3 0.2 copy.11
  8.4 0.9 pad_maximum_fusion.1
  9.3 3.1 broadcast_in_dim.18
  12.5 8.5 %all-to-all-start.1 = ((bf16[32,1280,80]{1,2,0:T(8,128)(2,1)}), bf16[32,1280,80]{1,2,0:T(8,128)(2,1)}, u32[]{:S(2)}, u32[]{:S(2)}) async-start(bf16[32,1280,80]{1,2,0:T(8,128)(2,1)} %broadcast_in_dim.18), calls=%async_computation.1 | async-start | bytes 13107200 | tf_op jit(solution)/shard_map/all_to_all | solution.py:50
  20.9 0.7 fusion.6
  21.6 9.0 %gather_fusion = bf16[32,40,3200]{2,1,0:T(8,128)(2,1)} fusion(bf16[32,40,3200]{2,1,0:T(8,128)(2,1)} %bitcast.23, s32[1024]{0:T(1024)S(1)} %pad_clamp_fusion), kind=kCustom, calls=%fused_computation | custom fusion | bytes 16384128 | tf_op jit(solution)/shard_map/jit(_take)/gather | solution.py:57
  30.6 0.7 compare_and_fusion
  31.3 98.2 %all-gather.3.cloned.1.call-done = bf16[3200,1280]{0,1:T(8,128)(2,1)} async-done(((bf16[3200,160]{0,1:T(8,128)(2,1)}), bf16[3200,1280]{0,1:T(8,128)(2,1)}) %all-gather.3.cloned.1.call-update) | async-done | bytes 8192016 | tf_op jit(solution)/shard_map/all_gather | solution.py:61
  129.5 17.8 %fusion = f32[32,40,1280]{2,1,0:T(8,128)} fusion(bf16[3200,1280]{0,1:T(8,128)(2,1)} %all-gather.3.cloned.1.call-done, bf16[32,40,3200]{2,1,0:T(8,128)(2,1)} %gather_fusion, pred[32]{0:T(512)(128)(4,1)S(1)} %compare_and_fusion), kind=kOutput, calls=%fused_computation.1 | convolution fusion | flops 10489856000 | bytes 22937632 | tf_op jit(solution)/shard_map/dot_general | solution.py:62
  147.3 14.3 %all-to-all-done.1 = bf16[32,1280,80]{1,2,0:T(8,128)(2,1)} async-done(((bf16[32,1280,80]{1,2,0:T(8,128)(2,1)}), bf16[32,1280,80]{1,2,0:T(8,128)(2,1)}, u32[]{:S(2)}, u32[]{:S(2)}) %all-to-all-start.1) | async-done | bytes 6553632 | tf_op jit(solution)/shard_map/all_to_all | solution.py:50
  161.7 9.5 %all-to-all-start = ((f32[32,40,1280]{2,1,0:T(8,128)}), f32[32,40,1280]{2,1,0:T(8,128)}, u32[]{:S(2)}, u32[]{:S(2)}) async-start(f32[32,40,1280]{2,1,0:T(8,128)} %fusion), calls=%async_computation | async-start | bytes 13107200 | tf_op jit(solution)/shard_map/all_to_all | solution.py:64
  171.2 0.0 all-gather.5.cloned.1.call-start
  171.2 1.3 dynamic_slice.10
  173.2 1.6 dynamic-slice_bitcast_fusion
  174.8 87.3 %all-to-all-done = f32[32,40,1280]{2,1,0:T(8,128)} async-done(((f32[32,40,1280]{2,1,0:T(8,128)}), f32[32,40,1280]{2,1,0:T(8,128)}, u32[]{:S(2)}, u32[]{:S(2)}) %all-to-all-start) | async-done | bytes 6553632 | tf_op jit(solution)/shard_map/all_to_all | solution.py:64
  262.1 3.2 reduce_sum.9
  265.3 0.2 copy.7
  265.5 0.1 subtract_convert_fusion
  265.6 0.1 pad_maximum_fusion
  265.8 0.2 copy.9
  266.0 17.3 %collective-permute-start = (bf16[40,2560]{1,0:T(8,128)(2,1)S(1)}, bf16[40,2560]{1,0:T(8,128)(2,1)S(1)}, u32[]{:S(2)}, u32[]{:S(2)}) collective-permute-start(bf16[40,2560]{1,0:T(8,128)(2,1)S(1)} %copy.9), channel_id=1, source_target_pairs={{0,0},{8,8},{16,16},{24,24},{32,17},{40,25},{48,1},{56,9},{64,14},... | collective-permute-start | bytes 614408 | tf_op jit(solution)/shard_map/ppermute | solution.py:74
  283.2 3.3 collective-permute-done
  286.5 0.0 copy-start
  286.5 0.7 copy-done
  287.2 0.0 all-gather.5.cloned.1.call-update
  287.2 40.9 %all-gather.5.cloned.1.call-done = bf16[320,2560]{1,0:T(8,128)(2,1)} async-done(((bf16[40,2560]{1,0:T(8,128)(2,1)}), bf16[320,2560]{1,0:T(8,128)(2,1)}) %all-gather.5.cloned.1.call-update) | async-done | bytes 1638416 | tf_op jit(solution)/shard_map/all_gather | solution.py:75
  328.1 3.6 %copy.10 = bf16[320,2560]{0,1:T(8,128)(2,1)S(1)} copy(bf16[320,2560]{1,0:T(8,128)(2,1)} %all-gather.5.cloned.1.call-done) | data formatting | bytes 3276800 | tf_op jit(solution)/shard_map/all_gather | solution.py:75
  331.7 6.8 %fusion.5 = f32[320,1280]{1,0:T(8,128)} fusion(f32[320,1280]{1,0:T(8,128)} %param.8, bf16[320,32,80]{0,2,1:T(8,128)(2,1)S(1)} %bitcast.22, bf16[32,1280,80]{1,2,0:T(8,128)(2,1)} %all-to-all-done.1), kind=kOutput, calls=%fused_computation.7 | convolution fusion | flops 2097561600 | bytes 11468800 | tf_op jit(solution)/shard_map/dot_general | solution.py:77
  (2 shorter events, 0.1 us)
Async XLA Ops:
  6.5 123.0 %all-gather.3.cloned.1.call-start = ((), (), s32[]{:S(2)}) async-start(), calls=%async_computation.2 | async-start | bytes 9216000 | tf_op jit(solution)/shard_map/all_gather | solution.py:61
  12.5 149.2 %all-to-all-start.1 = ((bf16[32,1280,80]{1,2,0:T(8,128)(2,1)}), bf16[32,1280,80]{1,2,0:T(8,128)(2,1)}, u32[]{:S(2)}, u32[]{:S(2)}) async-start(bf16[32,1280,80]{1,2,0:T(8,128)(2,1)} %broadcast_in_dim.18), calls=%async_computation.1 | async-start | bytes 13107200 | tf_op jit(solution)/shard_map/all_to_all | solution.py:50
  161.7 100.4 %all-to-all-start = ((f32[32,40,1280]{2,1,0:T(8,128)}), f32[32,40,1280]{2,1,0:T(8,128)}, u32[]{:S(2)}, u32[]{:S(2)}) async-start(f32[32,40,1280]{2,1,0:T(8,128)} %fusion), calls=%async_computation | async-start | bytes 13107200 | tf_op jit(solution)/shard_map/all_to_all | solution.py:64
  171.2 156.9 %all-gather.5.cloned.1.call-start = ((), (), s32[]{:S(2)}) async-start(), calls=%async_computation.3 | async-start | bytes 1843200 | tf_op jit(solution)/shard_map/all_gather | solution.py:75
  266.0 20.5 %collective-permute-start = (bf16[40,2560]{1,0:T(8,128)(2,1)S(1)}, bf16[40,2560]{1,0:T(8,128)(2,1)S(1)}, u32[]{:S(2)}, u32[]{:S(2)}) collective-permute-start(bf16[40,2560]{1,0:T(8,128)(2,1)S(1)} %copy.9), channel_id=1, source_target_pairs={{0,0},{8,8},{16,16},{24,24},{32,17},{40,25},{48,1},{56,9},{64,14},... | collective-permute-start | bytes 614408 | tf_op jit(solution)/shard_map/ppermute | solution.py:74
  286.5 0.7 copy-start
Sparse Core Ops, SparseCore 0:
  9.2 120.3 all-gather.2
  287.3 40.7 all-gather.4

commit v9 on v8

--- a/solution.py
+++ b/solution.py
@@ -72,11 +72,12 @@
 
     shape = left_piece.shape
     left_piece = lax.ppermute(left_piece.reshape(piece, -1), ("wide", "narrow"), perm)
-    left_rows = lax.all_gather(left_piece, "narrow", axis=0, tiled=True).reshape((tile_rows,) + shape[1:])
+    left_rows = lax.all_gather(left_piece, "narrow", axis=0, tiled=True)
 
+    right = jnp.transpose(rc_all, (1, 0, 2)).reshape(slope_rows, -1)
     update = lax.dot_general(
-        left_rows, rc_all, (((1, 2), (0, 2)), ((), ())), preferred_element_type=jnp.float32
-    )
+        right, left_rows, (((1,), (1,)), ((), ())), preferred_element_type=jnp.float32
+    ).T
     return cee_in + update
 
 

time: 348 us -> 344 us (0.989)
  local copies, waits for them, and re-layouts: 20.9 us -> 17.4 us
    all_gather x1 -> x0, local copies, waits for them, and re-layouts: 3.6 us -> none  [per_device(): lax.all_gather(left_piece, 'narrow', axis=0, tiled=True)]
where the time goes in v9:
time: 344 us; the launch traced here: 342 us
  waiting for transfers between devices  245 us (71%)
  starting transfers between devices  35.3 us (10%)
  matrix products  24.6 us (7%)
  local copies, waits for them, and re-layouts  17.4 us (5%)
  between operations  14.2 us (4%)
  other arithmetic  5.75 us (2%)
    all_gather x1, waiting for transfers between devices, per_device(): cmm_full = lax.all_gather(cmm_panel, 'narrow', axis=1, tiled=True)  98.2 us
    all_to_all x1, waiting for transfers between devices, per_device(): lax.all_to_all(z_part.reshape(n_wide, piece, z_part.shape[1]), 'wide', 0,...  87.2 us
    all_gather x1, waiting for transfers between devices, per_device(): left_rows = lax.all_gather(left_piece, 'narrow', axis=0, tiled=True)  40.2 us
    dot_general x1, matrix products, per_device(): z_part = jnp.dot(r_sent, cmm_full, preferred_element_type=jnp.float32)  17.8 us
    ppermute x1, starting transfers between devices, per_device(): lax.ppermute(left_piece.reshape(piece, -1), ('wide', 'narrow'), perm)  17.3 us
    all_to_all x1, waiting for transfers between devices, per_device(): lax.all_to_all(jnp.broadcast_to(rc[None], (n_wide,) + rc.shape), 'wide',...  14.3 us
    all_to_all x1, starting transfers between devices, per_device(): lax.all_to_all(z_part.reshape(n_wide, piece, z_part.shape[1]), 'wide', 0,...  9.53 us
    gather x1, local copies, waits for them, and re-layouts, per_device(): jnp.take(r_matrix.reshape(n_wide, piece, r_matrix.shape[1]), pieces[narro...  8.99 us
  transfers between devices with their start and end apart: 5, of which 5 were waited for; matrix products, arithmetic and copies ran while one was open for 11% of the time, Pallas kernels for 0%

profile of v9, /device:TPU:42, one launch (start us, length us, event | category | flops | bytes accessed | tf_op | source)
XLA Modules:
  0.0 341.8 jit_solution(3608485795724311662)
XLA Ops:
  6.5 0.0 all-gather.3.cloned.1.call-start
  6.5 0.7 all-gather.3.cloned.1.call-update
  7.3 1.0 slice.9
  8.3 0.2 copy.13
  8.4 0.9 pad_maximum_fusion.1
  9.3 3.1 broadcast_in_dim.18
  12.5 8.5 %all-to-all-start.1 = ((bf16[32,1280,80]{1,2,0:T(8,128)(2,1)}), bf16[32,1280,80]{1,2,0:T(8,128)(2,1)}, u32[]{:S(2)}, u32[]{:S(2)}) async-start(bf16[32,1280,80]{1,2,0:T(8,128)(2,1)} %broadcast_in_dim.18), calls=%async_computation.1 | async-start | bytes 13107200 | tf_op jit(solution)/shard_map/all_to_all | solution.py:50
  20.9 0.7 fusion.5
  21.6 9.0 %gather_fusion = bf16[32,40,3200]{2,1,0:T(8,128)(2,1)} fusion(bf16[32,40,3200]{2,1,0:T(8,128)(2,1)} %bitcast.20, s32[1024]{0:T(1024)S(1)} %pad_clamp_fusion), kind=kCustom, calls=%fused_computation | custom fusion | bytes 16384128 | tf_op jit(solution)/shard_map/jit(_take)/gather | solution.py:57
  30.6 0.7 compare_and_fusion
  31.3 98.2 %all-gather.3.cloned.1.call-done = bf16[3200,1280]{0,1:T(8,128)(2,1)} async-done(((bf16[3200,160]{0,1:T(8,128)(2,1)}), bf16[3200,1280]{0,1:T(8,128)(2,1)}) %all-gather.3.cloned.1.call-update) | async-done | bytes 8192016 | tf_op jit(solution)/shard_map/all_gather | solution.py:61
  129.5 17.8 %fusion = f32[32,40,1280]{2,1,0:T(8,128)} fusion(bf16[3200,1280]{0,1:T(8,128)(2,1)} %all-gather.3.cloned.1.call-done, bf16[32,40,3200]{2,1,0:T(8,128)(2,1)} %gather_fusion, pred[32]{0:T(512)(128)(4,1)S(1)} %compare_and_fusion), kind=kOutput, calls=%fused_computation.1 | convolution fusion | flops 10489856000 | bytes 22937632 | tf_op jit(solution)/shard_map/dot_general | solution.py:62
  147.3 14.3 %all-to-all-done.1 = bf16[32,1280,80]{1,2,0:T(8,128)(2,1)} async-done(((bf16[32,1280,80]{1,2,0:T(8,128)(2,1)}), bf16[32,1280,80]{1,2,0:T(8,128)(2,1)}, u32[]{:S(2)}, u32[]{:S(2)}) %all-to-all-start.1) | async-done | bytes 6553632 | tf_op jit(solution)/shard_map/all_to_all | solution.py:50
  161.6 9.5 %all-to-all-start = ((f32[32,40,1280]{2,1,0:T(8,128)}), f32[32,40,1280]{2,1,0:T(8,128)}, u32[]{:S(2)}, u32[]{:S(2)}) async-start(f32[32,40,1280]{2,1,0:T(8,128)} %fusion), calls=%async_computation | async-start | bytes 13107200 | tf_op jit(solution)/shard_map/all_to_all | solution.py:64
  171.2 0.0 all-gather.5.cloned.1.call-start
  171.2 1.3 dynamic_slice.10
  173.2 0.0 copy-start.1
  173.2 1.7 dynamic-slice_bitcast_fusion
  174.9 87.2 %all-to-all-done = f32[32,40,1280]{2,1,0:T(8,128)} async-done(((f32[32,40,1280]{2,1,0:T(8,128)}), f32[32,40,1280]{2,1,0:T(8,128)}, u32[]{:S(2)}, u32[]{:S(2)}) %all-to-all-start) | async-done | bytes 6553632 | tf_op jit(solution)/shard_map/all_to_all | solution.py:64
  262.1 3.2 reduce_sum.9
  265.3 0.2 copy.12
  265.5 0.1 subtract_convert_fusion
  265.6 0.1 pad_maximum_fusion
  265.7 0.2 copy.11
  266.0 17.3 %collective-permute-start = (bf16[40,2560]{1,0:T(8,128)(2,1)S(1)}, bf16[40,2560]{1,0:T(8,128)(2,1)S(1)}, u32[]{:S(2)}, u32[]{:S(2)}) collective-permute-start(bf16[40,2560]{1,0:T(8,128)(2,1)S(1)} %copy.11), channel_id=1, source_target_pairs={{0,0},{8,8},{16,16},{24,24},{32,17},{40,25},{48,1},{56,9},{64,14},... | collective-permute-start | bytes 614408 | tf_op jit(solution)/shard_map/ppermute | solution.py:74
  283.2 4.0 %collective-permute-done = bf16[40,2560]{1,0:T(8,128)(2,1)S(1)} collective-permute-done((bf16[40,2560]{1,0:T(8,128)(2,1)S(1)}, bf16[40,2560]{1,0:T(8,128)(2,1)S(1)}, u32[]{:S(2)}, u32[]{:S(2)}) %collective-permute-start) | collective-permute-done | bytes 204832 | tf_op jit(solution)/shard_map/ppermute | solution.py:74
  287.2 0.0 copy-start
  287.2 0.7 copy-done
  287.9 0.0 all-gather.5.cloned.1.call-update
  287.9 40.2 %all-gather.5.cloned.1.call-done = bf16[320,2560]{1,0:T(8,128)(2,1)} async-done(((bf16[40,2560]{1,0:T(8,128)(2,1)}), bf16[320,2560]{1,0:T(8,128)(2,1)}) %all-gather.5.cloned.1.call-update) | async-done | bytes 1638416 | tf_op jit(solution)/shard_map/all_gather | solution.py:75
  328.1 0.0 copy-done.1
  328.1 6.8 %convolution_add_fusion = f32[320,1280]{1,0:T(8,128)} fusion(f32[320,1280]{1,0:T(8,128)S(1)} %copy-done.1, bf16[320,2560]{1,0:T(8,128)(2,1)} %all-gather.5.cloned.1.call-done, bf16[1280,2560]{0,1:T(8,128)(2,1)} %bitcast.10), kind=kOutput, calls=%fused_computation.6 | convolution fusion | flops 2097561600 | bytes 11468800 | tf_op jit(solution)/shard_map/dot_general | solution.py:78
  (2 shorter events, 0.1 us)
Async XLA Ops:
  6.5 123.0 %all-gather.3.cloned.1.call-start = ((), (), s32[]{:S(2)}) async-start(), calls=%async_computation.2 | async-start | bytes 9216000 | tf_op jit(solution)/shard_map/all_gather | solution.py:61
  12.5 149.2 %all-to-all-start.1 = ((bf16[32,1280,80]{1,2,0:T(8,128)(2,1)}), bf16[32,1280,80]{1,2,0:T(8,128)(2,1)}, u32[]{:S(2)}, u32[]{:S(2)}) async-start(bf16[32,1280,80]{1,2,0:T(8,128)(2,1)} %broadcast_in_dim.18), calls=%async_computation.1 | async-start | bytes 13107200 | tf_op jit(solution)/shard_map/all_to_all | solution.py:50
  161.6 100.5 %all-to-all-start = ((f32[32,40,1280]{2,1,0:T(8,128)}), f32[32,40,1280]{2,1,0:T(8,128)}, u32[]{:S(2)}, u32[]{:S(2)}) async-start(f32[32,40,1280]{2,1,0:T(8,128)} %fusion), calls=%async_computation | async-start | bytes 13107200 | tf_op jit(solution)/shard_map/all_to_all | solution.py:64
  171.2 156.9 %all-gather.5.cloned.1.call-start = ((), (), s32[]{:S(2)}) async-start(), calls=%async_computation.3 | async-start | bytes 1843200 | tf_op jit(solution)/shard_map/all_gather | solution.py:75
  173.2 154.9 %copy-start.1 = (f32[320,1280]{1,0:T(8,128)S(1)}, f32[320,1280]{1,0:T(8,128)}, u32[]{:S(2)}) copy-start(f32[320,1280]{1,0:T(8,128)} %param.8) | copy-start | bytes 4915204
  266.0 21.3 %collective-permute-start = (bf16[40,2560]{1,0:T(8,128)(2,1)S(1)}, bf16[40,2560]{1,0:T(8,128)(2,1)S(1)}, u32[]{:S(2)}, u32[]{:S(2)}) collective-permute-start(bf16[40,2560]{1,0:T(8,128)(2,1)S(1)} %copy.11), channel_id=1, source_target_pairs={{0,0},{8,8},{16,16},{24,24},{32,17},{40,25},{48,1},{56,9},{64,14},... | collective-permute-start | bytes 614408 | tf_op jit(solution)/shard_map/ppermute | solution.py:74
  287.2 0.7 copy-start
Sparse Core Ops, SparseCore 0:
  9.2 120.3 all-gather.2
  288.1 40.0 all-gather.4
